TPU v7x, 512 devices: a whole 4x8x8 slice. The times are simulated.
512 devices in a mesh: group: 8 (over z_lo, core), dp: 8 (over y), tensor: 8 (over z_hi, x).
Axes of the slice: x: 4, y: 8, z: 8 (z_hi: 2, z_lo: 4; z = z_hi * 4 + z_lo), core: 2. Of those that a mesh axis runs over, the one named last changes fastest.
Arguments:
- keyvalue_local: float32 [8, 2, 4096, 1024], P('group', None, 'dp', 'tensor'), may hold values from -6 to 6
- keyvalue_anchor: float32 [2, 4096, 1024], P(None, 'dp', 'tensor'), may hold values from -6 to 6
- keyvalue_state: float32 [2, 4096, 1024], P(None, 'dp', 'tensor'), may hold values from -6 to 6
- router_local: float32 [8, 4096, 8], P('group', 'dp'), may hold values from -6 to 6
- router_anchor: float32 [4096, 8], P('dp'), may hold values from -6 to 6
- router_state: float32 [4096, 8], P('dp'), may hold values from -6 to 6
- gain_local: float32 [8, 2, 4096], P('group', None, 'dp'), may hold values from -6 to 6
- gain_anchor: float32 [2, 4096], P(None, 'dp'), may hold values from -6 to 6
- gain_state: float32 [2, 4096], P(None, 'dp'), may hold values from -6 to 6
- embed_local: float32 [8, 1000, 4096], P('group', 'dp', 'tensor'), may hold values from -6 to 6
- embed_anchor: float32 [1000, 4096], P('dp', 'tensor'), may hold values from -6 to 6
- embed_state: float32 [1000, 4096], P('dp', 'tensor'), may hold values from -6 to 6
- embed_basis: float32 [4096, 64], P('tensor'), may hold values from -0.25 to 0.25
- outer_rate: float32 [], replicated, may hold values from 0.5 to 1
Outputs:
- keyvalue_average: float32 [2, 4096, 1024], P(None, 'dp', 'tensor')
- keyvalue_momentum: float32 [2, 4096, 1024], P(None, 'dp', 'tensor')
- keyvalue_updated: float32 [2, 4096, 1024], P(None, 'dp', 'tensor')
- router_average: float32 [4096, 8], P('dp')
- router_momentum: float32 [4096, 8], P('dp')
- router_updated: float32 [4096, 8], P('dp')
- gain_average: float32 [2, 4096], P(None, 'dp')
- gain_momentum: float32 [2, 4096], P(None, 'dp')
- gain_updated: float32 [2, 4096], P(None, 'dp')
- embed_average: float32 [1000, 4096], P('dp', 'tensor')
- embed_momentum: float32 [1000, 4096], P('dp', 'tensor')
- embed_updated: float32 [1000, 4096], P('dp', 'tensor')
All inputs are finite; a program needn't handle non-finite values.
Results may differ from a plain program's by a relative error of at most 0.0001.
Values sent between devices are 32-bit elements; how exact they have to be, the bound alone decides.
No kernel may reach another device: no remote copies, remote signals or barrier semaphores. Data moves between devices by JAX's collectives and lax.ppermute only.
A program may use at most 64 MiB of HBM per device.

v0:
```python
import jax
import jax.numpy as jnp
from jax import lax
from jax.sharding import PartitionSpec as P


def nesterov(average, state, anchor, outer_rate):
    momentum = 0.5 * state + average
    updated = anchor - outer_rate * (average + 0.5 * momentum)
    return (average, momentum, updated)


def owned_slice(whole, position, count, axis_dim):
    return lax.dynamic_slice_in_dim(whole, position * count, count, axis_dim)


def local(
    keyvalue_local,
    keyvalue_anchor,
    keyvalue_state,
    router_local,
    router_anchor,
    router_state,
    gain_local,
    gain_anchor,
    gain_state,
    embed_local,
    embed_anchor,
    embed_state,
    embed_basis,
    outer_rate,
):
    groups = lax.axis_size("group")
    keyvalue_diff = keyvalue_anchor - keyvalue_local[0]
    router_diff = router_anchor - router_local[0]
    gain_diff = gain_anchor - gain_local[0]
    keyvalue_sum, router_sum, gain_sum = (
        lax.psum_scatter(keyvalue_diff, "group", scatter_dimension=1, tiled=True),
        lax.psum_scatter(router_diff, "group", scatter_dimension=0, tiled=True),
        lax.psum_scatter(gain_diff, "group", scatter_dimension=1, tiled=True),
    )
    position = lax.axis_index("group")
    keyvalue_rows = keyvalue_anchor.shape[1] // groups
    router_rows = router_anchor.shape[0] // groups
    gain_rows = gain_anchor.shape[1] // groups
    keyvalue_part = nesterov(
        keyvalue_sum / groups,
        owned_slice(keyvalue_state, position, keyvalue_rows, 1),
        owned_slice(keyvalue_anchor, position, keyvalue_rows, 1),
        outer_rate,
    )
    router_part = nesterov(
        router_sum / groups,
        owned_slice(router_state, position, router_rows, 0),
        owned_slice(router_anchor, position, router_rows, 0),
        outer_rate,
    )
    gain_part = nesterov(
        gain_sum / groups,
        owned_slice(gain_state, position, gain_rows, 1),
        owned_slice(gain_anchor, position, gain_rows, 1),
        outer_rate,
    )
    gathered = (
        lax.all_gather(keyvalue_part[0], "group", axis=1, tiled=True),
        lax.all_gather(keyvalue_part[1], "group", axis=1, tiled=True),
        lax.all_gather(keyvalue_part[2], "group", axis=1, tiled=True),
        lax.all_gather(router_part[0], "group", axis=0, tiled=True),
        lax.all_gather(router_part[1], "group", axis=0, tiled=True),
        lax.all_gather(router_part[2], "group", axis=0, tiled=True),
        lax.all_gather(gain_part[0], "group", axis=1, tiled=True),
        lax.all_gather(gain_part[1], "group", axis=1, tiled=True),
        lax.all_gather(gain_part[2], "group", axis=1, tiled=True),
    )
    keyvalue_out = gathered[0:3]
    router_out = gathered[3:6]
    gain_out = gathered[6:9]
    partial_factors = jnp.dot(
        embed_anchor - embed_local[0],
        embed_basis,
        precision=lax.Precision.HIGHEST,
        preferred_element_type=jnp.float32,
    )
    factors = lax.psum(partial_factors, ("group", "tensor"))
    factors = factors / groups
    embed_average = jnp.dot(
        factors, embed_basis.T, precision=lax.Precision.HIGHEST, preferred_element_type=jnp.float32
    )
    embed_out = nesterov(embed_average, embed_state, embed_anchor, outer_rate)
    return (
        keyvalue_out[0],
        keyvalue_out[1],
        keyvalue_out[2],
        router_out[0],
        router_out[1],
        router_out[2],
        gain_out[0],
        gain_out[1],
        gain_out[2],
        embed_out[0],
        embed_out[1],
        embed_out[2],
    )


def solution(mesh):
    in_specs = (
        P("group", None, "dp", "tensor"),
        P(None, "dp", "tensor"),
        P(None, "dp", "tensor"),
        P("group", "dp", None),
        P("dp", None),
        P("dp", None),
        P("group", None, "dp"),
        P(None, "dp"),
        P(None, "dp"),
        P("group", "dp", "tensor"),
        P("dp", "tensor"),
        P("dp", "tensor"),
        P("tensor", None),
        P(),
    )
    out_specs = (
        P(None, "dp", "tensor"),
        P(None, "dp", "tensor"),
        P(None, "dp", "tensor"),
        P("dp", None),
        P("dp", None),
        P("dp", None),
        P(None, "dp"),
        P(None, "dp"),
        P(None, "dp"),
        P("dp", "tensor"),
        P("dp", "tensor"),
        P("dp", "tensor"),
    )
    return jax.shard_map(local, mesh=mesh, in_specs=in_specs, out_specs=out_specs, check_vma=False)
```

profile of v0, /device:TPU:1, one launch (start us, length us, event | category | flops | bytes accessed | tf_op | source)
XLA Modules:
  0.0 506.9 jit_solution(6677557871619569564)
XLA Ops:
  7.3 0.7 bitcast_subtract_fusion.4
  8.0 0.9 copy.46
  9.0 0.8 copy.44
  9.9 0.8 bitcast_subtract_fusion
  11.5 0.2 copy-done.1
  11.7 0.1 copy-done.4
  11.8 0.4 fusion
  12.2 359.8 %psum.7 = f32[125,64]{0,1:T(8,128)S(1)} all-reduce(f32[125,64]{0,1:T(8,128)S(1)} %fusion), channel_id=1, replica_groups=mesh['group'=8,'dp'=8,'tensor'=8] {'group','tensor'}, use_global_device_ids=true, to_apply=%region_3.0 | all-reduce | flops 8000 | bytes 64000 | tf_op jit(solution)/shard_map/psum | solution.py:84
  372.0 1.3 multiply_subtract_fusion
  373.3 0.8 copy.47
  374.1 0.8 fusion.9
  374.9 10.7 %all-gather.5 = f32[8,64,2]{1,2,0:T(2,128)S(1)} all-gather(f32[1,64,2]{1,2,0:T(2,128)S(1)} %get-tuple-element.19), channel_id=1, replica_groups=mesh['group'=8,'dp'=8,'tensor'=8] {'group'}, dimensions={0}, use_global_device_ids=true | all-gather | bytes 4608 | tf_op jit(solution)/shard_map/all_gather | solution.py:73
  385.6 0.7 reshape.35
  386.3 8.7 %all-gather.4 = f32[8,64,2]{1,2,0:T(2,128)S(1)} all-gather(f32[1,64,2]{1,2,0:T(2,128)S(1)} %get-tuple-element.20), channel_id=1, replica_groups=mesh['group'=8,'dp'=8,'tensor'=8] {'group'}, dimensions={0}, use_global_device_ids=true | all-gather | bytes 4608 | tf_op jit(solution)/shard_map/all_gather | solution.py:72
  395.0 0.7 reshape.33
  395.7 10.1 %all-gather.3 = f32[8,64,2]{1,2,0:T(2,128)S(1)} all-gather(f32[1,64,2]{1,2,0:T(2,128)S(1)} %get-tuple-element.22), channel_id=1, replica_groups=mesh['group'=8,'dp'=8,'tensor'=8] {'group'}, dimensions={0}, use_global_device_ids=true | all-gather | bytes 4608 | tf_op jit(solution)/shard_map/all_gather | solution.py:71
  405.7 0.7 reshape.31
  406.4 0.8 copy.45
  407.2 0.8 subtract_bitcast_fusion
  408.0 14.1 %all-gather.2 = f32[8,64,8]{1,2,0:T(8,128)S(1)} all-gather(f32[1,64,8]{1,2,0:T(8,128)S(1)} %get-tuple-element.17), channel_id=1, replica_groups=mesh['group'=8,'dp'=8,'tensor'=8] {'group'}, dimensions={0}, use_global_device_ids=true | all-gather | bytes 18432 | tf_op jit(solution)/shard_map/all_gather | solution.py:70
  422.1 0.7 reshape.29
  422.8 14.1 %all-gather.1 = f32[8,64,8]{1,2,0:T(8,128)S(1)} all-gather(f32[1,64,8]{1,2,0:T(8,128)S(1)} %get-tuple-element.18), channel_id=1, replica_groups=mesh['group'=8,'dp'=8,'tensor'=8] {'group'}, dimensions={0}, use_global_device_ids=true | all-gather | bytes 18432 | tf_op jit(solution)/shard_map/all_gather | solution.py:69
  436.9 0.7 reshape.27
  437.5 14.1 %all-gather = f32[8,64,8]{1,2,0:T(8,128)S(1)} all-gather(f32[1,64,8]{1,2,0:T(8,128)S(1)} %get-tuple-element.21), channel_id=1, replica_groups=mesh['group'=8,'dp'=8,'tensor'=8] {'group'}, dimensions={0}, use_global_device_ids=true | all-gather | bytes 18432 | tf_op jit(solution)/shard_map/all_gather | solution.py:68
  451.6 0.7 reshape.25
  452.3 0.9 multiply_subtract_fusion.1
  453.2 14.9 %all_gather.29 = f32[2,512,128]{2,1,0:T(8,128)S(1)} all-gather(f32[2,64,128]{2,1,0:T(8,128)S(1)} %get-tuple-element.14), channel_id=1, replica_groups=mesh['group'=8,'dp'=8,'tensor'=8] {'group'}, dimensions={1}, use_global_device_ids=true | all-gather | bytes 589824 | tf_op jit(solution)/shard_map/all_gather | solution.py:67
  468.1 14.9 %all_gather.28 = f32[2,512,128]{2,1,0:T(8,128)S(1)} all-gather(f32[2,64,128]{2,1,0:T(8,128)S(1)} %get-tuple-element.15), channel_id=1, replica_groups=mesh['group'=8,'dp'=8,'tensor'=8] {'group'}, dimensions={1}, use_global_device_ids=true | all-gather | bytes 589824 | tf_op jit(solution)/shard_map/all_gather | solution.py:66
  483.0 14.9 %all_gather.27 = f32[2,512,128]{2,1,0:T(8,128)S(1)} all-gather(f32[2,64,128]{2,1,0:T(8,128)S(1)} %get-tuple-element.16), channel_id=1, replica_groups=mesh['group'=8,'dp'=8,'tensor'=8] {'group'}, dimensions={1}, use_global_device_ids=true | all-gather | bytes 589824 | tf_op jit(solution)/shard_map/all_gather | solution.py:65
  498.0 0.8 copy.57
  498.7 0.8 copy.58
  499.5 0.8 copy.59
  (30 shorter events, 0.2 us)
Async XLA Ops:
  7.2 4.3 copy-start
  7.2 366.1 %reduce-scatter.12.cloned.1.call-start = ((), (), s32[]{:S(2)}) async-start(), calls=%async_computation.5 | async-start | bytes 294912
  7.2 1.7 copy-start.6
  7.2 1.7 copy-start.7
  8.0 1.9 copy-start.2
  8.0 1.9 copy-start.3
  8.9 397.5 %reduce-scatter.10.cloned.1.call-start = ((), (), s32[]{:S(2)}) async-start(), calls=%async_computation.4 | async-start | bytes 294912
  9.8 442.5 %reduce-scatter.8.cloned.1.call-start = ((), (), s32[]{:S(2)}) async-start(), calls=%async_computation.3 | async-start | bytes 589824 | tf_op jit(solution)/shard_map/reduce_scatter | solution.py:38
  10.8 0.9 copy-start.1
  10.8 1.0 copy-start.4
  11.8 360.2 %copy-start.5 = (f32[125,512]{1,0:T(8,128)S(1)}, f32[125,512]{1,0:T(8,128)}, u32[]{:S(2)}) copy-start(f32[125,512]{1,0:T(8,128)} %param.25) | copy-start | bytes 768004
Sparse Core Ops, SparseCore 0:
  11.4 42.3 reduce-scatter.11
  57.1 37.8 reduce-scatter.9
  98.4 38.6 reduce-scatter.7
where the time goes:
time: 512 us; the launch traced here: 507 us
  blocking collectives  476 us (93%)
  between operations  14.6 us (3%)
  local copies, waits for them, and re-layouts  10.1 us (2%)
    psum x1, blocking collectives, local(): factors = lax.psum(partial_factors, ('group', 'tensor'))  360 us
    all_gather x1, blocking collectives, local(): lax.all_gather(keyvalue_part[2], 'group', axis=1, tiled=True)  14.9 us
    all_gather x1, blocking collectives, local(): lax.all_gather(keyvalue_part[1], 'group', axis=1, tiled=True)  14.9 us
    all_gather x1, blocking collectives, local(): lax.all_gather(keyvalue_part[0], 'group', axis=1, tiled=True)  14.9 us
    all_gather x1, blocking collectives, local(): lax.all_gather(router_part[2], 'group', axis=0, tiled=True)  14.1 us
    all_gather x1, blocking collectives, local(): lax.all_gather(router_part[1], 'group', axis=0, tiled=True)  14.1 us
    all_gather x1, blocking collectives, local(): lax.all_gather(router_part[0], 'group', axis=0, tiled=True)  14.1 us
    all_gather x1, blocking collectives, local(): lax.all_gather(gain_part[2], 'group', axis=1, tiled=True)  10.7 us
  transfers between devices with their start and end apart: 3, of which 0 were waited for; matrix products, arithmetic and copies ran while one was open for 2% of the time, Pallas kernels for 0%

commit v1 on v0

v1 whole, which is shorter than its diff:
```python
import jax
import jax.numpy as jnp
from jax import lax
from jax.sharding import PartitionSpec as P

HIGHEST = lax.Precision.HIGHEST
MODE = "separate"


def nesterov(average, state, anchor, outer_rate):
    momentum = 0.5 * state + average
    updated = anchor - outer_rate * (average + 0.5 * momentum)
    return (average, momentum, updated)


def local(kv_local, kv_anchor, kv_state, r_local, r_anchor, r_state, g_local, g_anchor, g_state,
          e_local, e_anchor, e_state, basis, rate):
    groups = lax.axis_size("group")
    kv_diff = kv_anchor - kv_local[0]
    r_diff = r_anchor - r_local[0]
    g_diff = g_anchor - g_local[0]
    partial = jnp.dot(e_anchor - e_local[0], basis, precision=HIGHEST, preferred_element_type=jnp.float32)
    if MODE == "concat":
        partial = lax.psum(partial, "tensor")
        pieces = (kv_diff, r_diff, g_diff, partial)
        flat = jnp.concatenate([p.reshape(-1) for p in pieces])
        total = lax.psum(flat, "group")
        sums, at = [], 0
        for p in pieces:
            sums.append(total[at:at + p.size].reshape(p.shape))
            at += p.size
        kv_sum, r_sum, g_sum, factors = sums
    elif MODE == "separate":
        partial = lax.psum(partial, "tensor")
        kv_sum, r_sum, g_sum, factors = lax.psum((kv_diff, r_diff, g_diff, partial), "group")
    elif MODE == "nested":
        kv_sum, r_sum, g_sum = lax.psum((kv_diff, r_diff, g_diff), "group")
        factors = lax.psum(lax.psum(partial, "tensor"), "group")
    kv_out = nesterov(kv_sum / groups, kv_state, kv_anchor, rate)
    r_out = nesterov(r_sum / groups, r_state, r_anchor, rate)
    g_out = nesterov(g_sum / groups, g_state, g_anchor, rate)
    factors = factors / groups
    e_avg = jnp.dot(factors, basis.T, precision=HIGHEST, preferred_element_type=jnp.float32)
    e_out = nesterov(e_avg, e_state, e_anchor, rate)
    return (*kv_out, *r_out, *g_out, *e_out)


IN_SPECS = (
    P("group", None, "dp", "tensor"), P(None, "dp", "tensor"), P(None, "dp", "tensor"),
    P("group", "dp", None), P("dp", None), P("dp", None),
    P("group", None, "dp"), P(None, "dp"), P(None, "dp"),
    P("group", "dp", "tensor"), P("dp", "tensor"), P("dp", "tensor"),
    P("tensor", None), P(),
)
OUT_SPECS = (
    P(None, "dp", "tensor"), P(None, "dp", "tensor"), P(None, "dp", "tensor"),
    P("dp", None), P("dp", None), P("dp", None),
    P(None, "dp"), P(None, "dp"), P(None, "dp"),
    P("dp", "tensor"), P("dp", "tensor"), P("dp", "tensor"),
)


def solution(mesh):
    return jax.shard_map(local, mesh=mesh, in_specs=IN_SPECS, out_specs=OUT_SPECS, check_vma=False)
```

time: 512 us -> 108 us (0.21)
  the two profiles are of different devices: /device:TPU:1 before, /device:TPU:32 now
where the time goes in v1:
time: 108 us
  blocking collectives  85.4 us (79%)
  between operations  14.9 us (14%)
  other arithmetic  5.61 us (5%)
  matrix products  1.64 us (2%)
    psum x1, blocking collectives, local(): partial = lax.psum(partial, 'tensor')  58.1 us
    psum x1, blocking collectives, local(): lax.psum((kv_diff, r_diff, g_diff, partial), 'group')  27.3 us
    sub x3, other arithmetic, nesterov(): updated = anchor - outer_rate * (average + 0.5 * momentum)  3.52 us
  transfers between devices with their start and end apart: 1, of which 0 were waited for; matrix products, arithmetic and copies ran while one was open for 3% of the time, Pallas kernels for 0%

profile of v1, /device:TPU:32, one launch (start us, length us, event | category | flops | bytes accessed | tf_op | source)
XLA Modules:
  0.0 108.0 jit_solution(13273733922246938453)
XLA Ops:
  7.2 0.0 copy-start
  7.2 0.0 all-reduce.3.cloned.1.call-start
  7.2 2.1 %bitcast_subtract_fusion = f32[2,512,128]{2,1,0:T(8,128)} fusion(f32[2,512,128]{2,1,0:T(8,128)} %param.15, f32[1,2,512,128]{3,2,1,0:T(8,128)} %param.14), kind=kLoop, calls=%fused_computation | loop fusion | flops 131072 | bytes 1572864 | tf_op jit(solution)/shard_map/sub | solution.py:19
  9.3 0.0 copy-start.2
  9.3 0.0 copy-start.4
  9.3 0.0 all-reduce.3.cloned.1.call-update
  10.0 0.0 copy-done
  10.1 0.2 copy-done.2
  10.3 0.1 copy-done.4
  10.4 0.0 copy-start.6
  10.4 0.0 copy-start.7
  10.4 0.0 copy-start.8
  10.4 0.0 copy-start.10
  10.4 0.4 fusion
  10.7 0.0 copy-start.5
  10.8 58.1 %psum.38 = f32[125,64]{1,0:T(8,128)S(1)} all-reduce(f32[125,64]{1,0:T(8,128)S(1)} %fusion), channel_id=1, replica_groups=mesh['group'=8,'dp'=8,'tensor'=8] {'tensor'}, use_global_device_ids=true, to_apply=%region_3.0 | all-reduce | flops 8000 | bytes 64000 | tf_op jit(solution)/shard_map/psum | solution.py:34
  68.9 0.0 copy-done.6
  68.9 0.0 copy-done.7
  68.9 0.0 copy-done.8
  68.9 0.0 copy-done.10
  68.9 0.0 copy-start.11
  68.9 27.3 %all-reduce = (f32[512,8]{0,1:T(8,128)S(1)}, f32[2,512]{1,0:T(2,128)S(1)}, f32[125,64]{1,0:T(8,128)S(1)}) all-reduce(f32[512,8]{0,1:T(8,128)S(1)} %bitcast_subtract_fusion.3, f32[2,512]{1,0:T(2,128)S(1)} %bitcast_subtract_fusion.4, f32[125,64]{1,0:T(8,128)S(1)} %psum.38), channel_id=1, replica_groups=mesh['group'=8,'dp'=8,'tensor'=8] {'group'}, use_global_device_ids=true, to_apply=%region_1.0 | all-reduce | flops 13120 | bytes 104960 | tf_op jit(solution)/shard_map/psum | solution.py:35
  96.3 0.0 copy-start.9
  96.3 0.0 copy-done.11
  96.3 0.6 multiply_subtract_fusion.3
  96.9 0.1 copy-done.9
  97.0 0.6 multiply_subtract_fusion.2
  97.6 0.0 copy-done.5
  97.6 1.3 %multiply_subtract_fusion.1 = (f32[125,512]{1,0:T(8,128)}, f32[125,512]{1,0:T(8,128)}, f32[125,512]{1,0:T(8,128)}) fusion(f32[125,512]{1,0:T(8,128)S(1)} %copy-done.2, f32[]{:T(128)S(6)} %copy.32, f32[125,512]{1,0:T(8,128)S(1)} %copy-done.5, f32[512,64]{0,1:T(8,128)S(1)} %copy-done, f32[125,64]{1,0:T(8,128)S(1)} %get-tuple-element.14), kind=kOutput, calls=%fused_computation.6 | convolution fusion | flops 49544000 | bytes 1443076 | tf_op jit(solution)/shard_map/dot_general | solution.py:43
  98.9 0.0 copy-done.1
  98.9 0.0 copy-done.3
  98.9 2.3 %multiply_subtract_fusion = (f32[2,512,128]{2,1,0:T(8,128)}, f32[2,512,128]{2,1,0:T(8,128)}, f32[2,512,128]{2,1,0:T(8,128)}) fusion(f32[2,512,128]{2,1,0:T(8,128)S(1)} %copy-done.1, f32[]{:T(128)S(6)} %copy.32, f32[2,512,128]{2,1,0:T(8,128)S(1)} %copy-done.3, f32[2,512,128]{2,1,0:T(8,128)} %all-reduce.3.cloned.1.call-done), kind=kLoop, calls=%fused_computation.1 | loop fusion | flops 917504 | bytes 3145732 | tf_op jit(solution)/shard_map/sub | solution.py:12
  (5 shorter events, 0.0 us)
Async XLA Ops:
  7.2 2.9 %copy-start = (f32[512,64]{0,1:T(8,128)S(1)}, f32[512,64]{0,1:T(8,128)}, u32[]{:S(2)}) copy-start(f32[512,64]{0,1:T(8,128)} %param.26) | copy-start | bytes 393220
  7.2 91.7 %all-reduce.3.cloned.1.call-start = ((), (), s32[]{:S(2)}) async-start(), calls=%async_computation | async-start | bytes 1048576 | tf_op jit(solution)/shard_map/psum | solution.py:35
  9.3 1.0 copy-start.2
  9.3 1.0 copy-start.4
  10.4 58.5 %copy-start.6 = (f32[512,8]{0,1:T(8,128)S(1)}, f32[512,8]{0,1:T(8,128)}, u32[]{:S(2)}) copy-start(f32[512,8]{0,1:T(8,128)} %param.18) | copy-start | bytes 49156
  10.4 58.5 %copy-start.7 = (f32[1,512,8]{1,2,0:T(8,128)S(1)}, f32[1,512,8]{1,2,0:T(8,128)}, u32[]{:S(2)}) copy-start(f32[1,512,8]{1,2,0:T(8,128)} %param.17) | copy-start | bytes 49156
  10.4 58.5 %copy-start.8 = (f32[2,512]{1,0:T(2,128)S(1)}, f32[2,512]{1,0:T(2,128)}, u32[]{:S(2)}) copy-start(f32[2,512]{1,0:T(2,128)} %param.21) | copy-start | bytes 12292
  10.4 58.5 %copy-start.10 = (f32[1,2,512]{2,1,0:T(2,128)S(1)}, f32[1,2,512]{2,1,0:T(2,128)}, u32[]{:S(2)}) copy-start(f32[1,2,512]{2,1,0:T(2,128)} %param.20) | copy-start | bytes 12292
  10.7 86.9 %copy-start.5 = (f32[125,512]{1,0:T(8,128)S(1)}, f32[125,512]{1,0:T(8,128)}, u32[]{:S(2)}) copy-start(f32[125,512]{1,0:T(8,128)} %param.25) | copy-start | bytes 768004
  68.9 27.3 %copy-start.11 = (f32[2,512]{1,0:T(2,128)S(1)}, f32[2,512]{1,0:T(2,128)}, u32[]{:S(2)}) copy-start(f32[2,512]{1,0:T(2,128)} %param.22) | copy-start | bytes 12292
  96.3 0.7 copy-start.9
  97.6 1.3 %copy-start.1 = (f32[2,512,128]{2,1,0:T(8,128)S(1)}, f32[2,512,128]{2,1,0:T(8,128)}, u32[]{:S(2)}) copy-start(f32[2,512,128]{2,1,0:T(8,128)} %param.15) | copy-start | bytes 1572868
  97.6 1.3 %copy-start.3 = (f32[2,512,128]{2,1,0:T(8,128)S(1)}, f32[2,512,128]{2,1,0:T(8,128)}, u32[]{:S(2)}) copy-start(f32[2,512,128]{2,1,0:T(8,128)} %param.16) | copy-start | bytes 1572868
Sparse Core Ops, SparseCore 0:
  11.5 82.3 all-reduce.2

commit v2 on v1

--- a/solution.py
+++ b/solution.py
@@ -4,7 +4,7 @@
 from jax.sharding import PartitionSpec as P
 
 HIGHEST = lax.Precision.HIGHEST
-MODE = "separate"
+KV_MODE = "butterfly"
 
 
 def nesterov(average, state, anchor, outer_rate):
@@ -13,29 +13,60 @@
     return (average, momentum, updated)
 
 
+def flip(axis, bit):
+    n = lax.axis_size(axis)
+    return [(i, i ^ (1 << bit)) for i in range(n)]
+
+
+def all_reduce_doubling(x, steps):
+    for axis, bit in steps:
+        x = x + lax.ppermute(x, axis, flip(axis, bit))
+    return x
+
+
+def reduce_scatter_halving(x, axis, bits):
+    idx = lax.axis_index(axis)
+    for bit in bits:
+        half = x.shape[0] // 2
+        b = (idx >> bit) & 1
+        keep = lax.dynamic_slice_in_dim(x, b * half, half)
+        send = lax.dynamic_slice_in_dim(x, (1 - b) * half, half)
+        x = keep + lax.ppermute(send, axis, flip(axis, bit))
+    return x
+
+
+def all_gather_doubling(x, axis, bits):
+    idx = lax.axis_index(axis)
+    for bit in bits:
+        b = ((idx >> bit) & 1) == 0
+        other = lax.ppermute(x, axis, flip(axis, bit))
+        x = jnp.concatenate([jnp.where(b, x, other), jnp.where(b, other, x)])
+    return x
+
+
 def local(kv_local, kv_anchor, kv_state, r_local, r_anchor, r_state, g_local, g_anchor, g_state,
           e_local, e_anchor, e_state, basis, rate):
     groups = lax.axis_size("group")
+    group_bits = groups.bit_length() - 1
+    tensor_bits = lax.axis_size("tensor").bit_length() - 1
     kv_diff = kv_anchor - kv_local[0]
     r_diff = r_anchor - r_local[0]
     g_diff = g_anchor - g_local[0]
     partial = jnp.dot(e_anchor - e_local[0], basis, precision=HIGHEST, preferred_element_type=jnp.float32)
-    if MODE == "concat":
-        partial = lax.psum(partial, "tensor")
-        pieces = (kv_diff, r_diff, g_diff, partial)
-        flat = jnp.concatenate([p.reshape(-1) for p in pieces])
+    steps = [("group", b) for b in range(group_bits)] + [("tensor", b) for b in range(tensor_bits)]
+    factors = all_reduce_doubling(partial, steps)
+    pieces = (kv_diff, r_diff, g_diff)
+    flat = jnp.concatenate([p.reshape(-1) for p in pieces])
+    if KV_MODE == "butterfly":
+        bits = list(range(group_bits))
+        total = all_gather_doubling(reduce_scatter_halving(flat, "group", bits), "group", bits[::-1])
+    else:
         total = lax.psum(flat, "group")
-        sums, at = [], 0
-        for p in pieces:
-            sums.append(total[at:at + p.size].reshape(p.shape))
-            at += p.size
-        kv_sum, r_sum, g_sum, factors = sums
-    elif MODE == "separate":
-        partial = lax.psum(partial, "tensor")
-        kv_sum, r_sum, g_sum, factors = lax.psum((kv_diff, r_diff, g_diff, partial), "group")
-    elif MODE == "nested":
-        kv_sum, r_sum, g_sum = lax.psum((kv_diff, r_diff, g_diff), "group")
-        factors = lax.psum(lax.psum(partial, "tensor"), "group")
+    sums, at = [], 0
+    for p in pieces:
+        sums.append(total[at:at + p.size].reshape(p.shape))
+        at += p.size
+    kv_sum, r_sum, g_sum = sums
     kv_out = nesterov(kv_sum / groups, kv_state, kv_anchor, rate)
     r_out = nesterov(r_sum / groups, r_state, r_anchor, rate)
     g_out = nesterov(g_sum / groups, g_state, g_anchor, rate)

time: 108 us -> 79.9 us (0.74)
  the two profiles are of different devices: /device:TPU:32 before, /device:TPU:1 now
where the time goes in v2:
time: 79.9 us; the launch traced here: 79.2 us
  starting transfers between devices  49.4 us (62%)
  waiting for transfers between devices  19.1 us (24%)
  other arithmetic  5.51 us (7%)
  local copies, waits for them, and re-layouts  1.82 us (2%)
  between operations  1.74 us (2%)
  matrix products  1.73 us (2%)
    ppermute x6, starting transfers between devices, all_reduce_doubling(): x = x + lax.ppermute(x, axis, flip(axis, bit))  24.6 us
    ppermute x3, starting transfers between devices, reduce_scatter_halving(): x = keep + lax.ppermute(send, axis, flip(axis, bit))  12.6 us
    ppermute x3, starting transfers between devices, all_gather_doubling(): other = lax.ppermute(x, axis, flip(axis, bit))  12.2 us
    ppermute x3, waiting for transfers between devices, reduce_scatter_halving(): x = keep + lax.ppermute(send, axis, flip(axis, bit))  10.7 us
    ppermute x6, waiting for transfers between devices, all_reduce_doubling(): x = x + lax.ppermute(x, axis, flip(axis, bit))  8.35 us
    sub x3, other arithmetic, nesterov(): updated = anchor - outer_rate * (average + 0.5 * momentum)  2.29 us
  transfers between devices with their start and end apart: 12, of which 7 were waited for; matrix products, arithmetic and copies ran while one was open for 2% of the time, Pallas kernels for 0%

profile of v2, /device:TPU:1, one launch (start us, length us, event | category | flops | bytes accessed | tf_op | source)
XLA Modules:
  0.0 79.2 jit_solution(7762357851812091375)
XLA Ops:
  0.7 0.8 fusion.7
  1.5 0.7 bitcast_subtract_fusion.3
  2.3 0.2 reshape.59
  2.5 1.1 %bitcast_subtract_fusion = f32[2,512,128]{2,1,0:T(8,128)S(1)} fusion(f32[2,512,128]{2,1,0:T(8,128)S(1)} %copy-done.1, f32[1,2,512,128]{3,2,1,0:T(8,128)} %param.14), kind=kLoop, calls=%fused_computation.3 | loop fusion | flops 131072 | bytes 1572864 | tf_op jit(solution)/shard_map/sub | solution.py:52
  3.7 0.1 dynamic_slice.19
  3.8 8.7 %collective-permute-start = (f32[68096]{0:T(1024)S(1)}, f32[68096]{0:T(1024)S(1)}, u32[]{:S(2)}, u32[]{:S(2)}) collective-permute-start(f32[68096]{0:T(1024)S(1)} %dynamic_slice.19), channel_id=1, source_target_pairs={{0,64},{64,0},{128,192},{192,128},{256,320},{320,256},{384,448},{4... | collective-permute-start | bytes 817160 | tf_op jit(solution)/shard_map/ppermute | solution.py:34
  12.6 1.1 %collective-permute-done = f32[68096]{0:T(1024)S(1)} collective-permute-done((f32[68096]{0:T(1024)S(1)}, f32[68096]{0:T(1024)S(1)}, u32[]{:S(2)}, u32[]{:S(2)}) %collective-permute-start) | collective-permute-done | bytes 272416 | tf_op jit(solution)/shard_map/ppermute | solution.py:34
  14.0 1.9 %collective-permute-start.1 = (f32[34048]{0:T(1024)S(1)}, f32[34048]{0:T(1024)S(1)}, u32[]{:S(2)}, u32[]{:S(2)}) collective-permute-start(f32[34048]{0:T(1024)S(1)} %dynamic_slice.21), channel_id=1, source_target_pairs={{0,128},{64,192},{128,0},{192,64},{256,384},{320,448},{384,256},{4... | collective-permute-start | bytes 408584 | tf_op jit(solution)/shard_map/ppermute | solution.py:34
  15.9 4.8 %collective-permute-done.1 = f32[34048]{0:T(1024)S(1)} collective-permute-done((f32[34048]{0:T(1024)S(1)}, f32[34048]{0:T(1024)S(1)}, u32[]{:S(2)}, u32[]{:S(2)}) %collective-permute-start.1) | collective-permute-done | bytes 136224 | tf_op jit(solution)/shard_map/ppermute | solution.py:34
  21.0 1.9 %collective-permute-start.2 = (f32[17024]{0:T(1024)S(1)}, f32[17024]{0:T(1024)S(1)}, u32[]{:S(2)}, u32[]{:S(2)}) collective-permute-start(f32[17024]{0:T(1024)S(1)} %dynamic_slice.23), channel_id=1, source_target_pairs={{0,256},{64,320},{128,384},{192,448},{256,0},{320,64},{384,128},{4... | collective-permute-start | bytes 204296 | tf_op jit(solution)/shard_map/ppermute | solution.py:34
  22.9 4.8 %collective-permute-done.2 = f32[17024]{0:T(1024)S(1)} collective-permute-done((f32[17024]{0:T(1024)S(1)}, f32[17024]{0:T(1024)S(1)}, u32[]{:S(2)}, u32[]{:S(2)}) %collective-permute-start.2) | collective-permute-done | bytes 68128 | tf_op jit(solution)/shard_map/ppermute | solution.py:34
  27.8 1.9 %collective-permute-start.3 = (f32[17024]{0:T(1024)S(1)}, f32[17024]{0:T(1024)S(1)}, u32[]{:S(2)}, u32[]{:S(2)}) collective-permute-start(f32[17024]{0:T(1024)S(1)} %dynamic-slice_add_fusion.2), channel_id=1, source_target_pairs={{0,256},{64,320},{128,384},{192,448},{256,0},{320,64},{384,128},{4... | collective-permute-start | bytes 204296 | tf_op jit(solution)/shard_map/ppermute | solution.py:42
  29.7 0.4 fusion.1
  30.1 4.1 %collective-permute-start.6 = (f32[125,64]{0,1:T(8,128)S(1)}, f32[125,64]{0,1:T(8,128)S(1)}, u32[]{:S(2)}, u32[]{:S(2)}) collective-permute-start(f32[125,64]{0,1:T(8,128)S(1)} %fusion.1), channel_id=1, source_target_pairs={{0,64},{64,0},{128,192},{192,128},{256,320},{320,256},{384,448},{4... | collective-permute-start | bytes 96008 | tf_op jit(solution)/shard_map/ppermute | solution.py:23
  34.3 3.0 %collective-permute-start.4 = (f32[34048]{0:T(1024)S(1)}, f32[34048]{0:T(1024)S(1)}, u32[]{:S(2)}, u32[]{:S(2)}) collective-permute-start(f32[34048]{0:T(1024)S(1)} %pad_maximum_fusion.3), channel_id=1, source_target_pairs={{0,128},{64,192},{128,0},{192,64},{256,384},{320,448},{384,256},{4... | collective-permute-start | bytes 408584 | tf_op jit(solution)/shard_map/ppermute | solution.py:42
  37.3 2.3 %collective-permute-start.7 = (f32[125,64]{0,1:T(8,128)S(1)}, f32[125,64]{0,1:T(8,128)S(1)}, u32[]{:S(2)}, u32[]{:S(2)}) collective-permute-start(f32[125,64]{0,1:T(8,128)S(1)} %add.84), channel_id=1, source_target_pairs={{0,128},{64,192},{128,0},{192,64},{256,384},{320,448},{384,256},{4... | collective-permute-start | bytes 96008 | tf_op jit(solution)/shard_map/ppermute | solution.py:23
  39.6 2.8 %collective-permute-done.7 = f32[125,64]{0,1:T(8,128)S(1)} collective-permute-done((f32[125,64]{0,1:T(8,128)S(1)}, f32[125,64]{0,1:T(8,128)S(1)}, u32[]{:S(2)}, u32[]{:S(2)}) %collective-permute-start.7) | collective-permute-done | bytes 32032 | tf_op jit(solution)/shard_map/ppermute | solution.py:23
  42.4 4.2 %collective-permute-start.8 = (f32[125,64]{0,1:T(8,128)S(1)}, f32[125,64]{0,1:T(8,128)S(1)}, u32[]{:S(2)}, u32[]{:S(2)}) collective-permute-start(f32[125,64]{0,1:T(8,128)S(1)} %add.85), channel_id=1, source_target_pairs={{0,256},{64,320},{128,384},{192,448},{256,0},{320,64},{384,128},{4... | collective-permute-start | bytes 96008 | tf_op jit(solution)/shard_map/ppermute | solution.py:23
  46.6 1.3 %collective-permute-done.8 = f32[125,64]{0,1:T(8,128)S(1)} collective-permute-done((f32[125,64]{0,1:T(8,128)S(1)}, f32[125,64]{0,1:T(8,128)S(1)}, u32[]{:S(2)}, u32[]{:S(2)}) %collective-permute-start.8) | collective-permute-done | bytes 32032 | tf_op jit(solution)/shard_map/ppermute | solution.py:23
  47.9 2.5 %collective-permute-start.9 = (f32[125,64]{0,1:T(8,128)S(1)}, f32[125,64]{0,1:T(8,128)S(1)}, u32[]{:S(2)}, u32[]{:S(2)}) collective-permute-start(f32[125,64]{0,1:T(8,128)S(1)} %add.86), channel_id=1, source_target_pairs={{0,1},{1,0},{2,3},{3,2},{4,5},{5,4},{6,7},{7,6},{8,9},{9,8},{10,11... | collective-permute-start | bytes 96008 | tf_op jit(solution)/shard_map/ppermute | solution.py:23
  50.5 2.1 %collective-permute-done.9 = f32[125,64]{0,1:T(8,128)S(1)} collective-permute-done((f32[125,64]{0,1:T(8,128)S(1)}, f32[125,64]{0,1:T(8,128)S(1)}, u32[]{:S(2)}, u32[]{:S(2)}) %collective-permute-start.9) | collective-permute-done | bytes 32032 | tf_op jit(solution)/shard_map/ppermute | solution.py:23
  52.6 4.0 %collective-permute-start.10 = (f32[125,64]{0,1:T(8,128)S(1)}, f32[125,64]{0,1:T(8,128)S(1)}, u32[]{:S(2)}, u32[]{:S(2)}) collective-permute-start(f32[125,64]{0,1:T(8,128)S(1)} %add.87), channel_id=1, source_target_pairs={{0,2},{1,3},{2,0},{3,1},{4,6},{5,7},{6,4},{7,5},{8,10},{9,11},{10,... | collective-permute-start | bytes 96008 | tf_op jit(solution)/shard_map/ppermute | solution.py:23
  56.7 2.1 %collective-permute-done.10 = f32[125,64]{0,1:T(8,128)S(1)} collective-permute-done((f32[125,64]{0,1:T(8,128)S(1)}, f32[125,64]{0,1:T(8,128)S(1)}, u32[]{:S(2)}, u32[]{:S(2)}) %collective-permute-start.10) | collective-permute-done | bytes 32032 | tf_op jit(solution)/shard_map/ppermute | solution.py:23
  58.8 7.5 %collective-permute-start.11 = (f32[125,64]{0,1:T(8,128)S(1)}, f32[125,64]{0,1:T(8,128)S(1)}, u32[]{:S(2)}, u32[]{:S(2)}) collective-permute-start(f32[125,64]{0,1:T(8,128)S(1)} %add.88), channel_id=1, source_target_pairs={{0,4},{1,5},{2,6},{3,7},{4,0},{5,1},{6,2},{7,3},{8,12},{9,13},{10,... | collective-permute-start | bytes 96008 | tf_op jit(solution)/shard_map/ppermute | solution.py:23
  66.4 7.2 %collective-permute-start.5 = (f32[68096]{0:T(1024)S(1)}, f32[68096]{0:T(1024)S(1)}, u32[]{:S(2)}, u32[]{:S(2)}) collective-permute-start(f32[68096]{0:T(1024)S(1)} %pad_maximum_fusion.2), channel_id=1, source_target_pairs={{0,64},{64,0},{128,192},{192,128},{256,320},{320,256},{384,448},{4... | collective-permute-start | bytes 817160 | tf_op jit(solution)/shard_map/ppermute | solution.py:42
  74.3 1.3 %multiply_subtract_fusion.1 = (f32[125,512]{1,0:T(8,128)}, f32[125,512]{1,0:T(8,128)}, f32[125,512]{1,0:T(8,128)}) fusion(f32[125,512]{1,0:T(8,128)S(1)} %copy-done.3, f32[]{:T(128)S(6)} %copy.43, f32[125,512]{1,0:T(8,128)S(1)} %copy-done.6, f32[512,64]{0,1:T(8,128)S(1)} %copy-done, f32[125,64]{0,1:T(8,128)S(1)} %add.88, ...), kind=kOutput, calls=%fused_computation.11 | convolution fusion | flops 49552000 | bytes 1475076 | tf_op jit(solution)/shard_map/dot_general | solution.py:74
  75.8 0.2 div.35
  76.1 0.2 copy-done.11
  76.3 0.5 copy-done.10
  76.8 0.6 multiply_subtract_fusion.3
  77.5 0.6 multiply_subtract_fusion.2
  78.2 1.1 %multiply_subtract_fusion = (f32[2,512,128]{2,1,0:T(8,128)}, f32[2,512,128]{2,1,0:T(8,128)}) fusion(f32[2,512,128]{2,1,0:T(8,128)S(1)} %copy-done.1, f32[2,512,128]{2,1,0:T(8,128)S(1)} %bitcast.19, f32[]{:T(128)S(6)} %copy.43, f32[2,512,128]{2,1,0:T(8,128)S(1)} %copy-done.4), kind=kLoop, calls=%fused_computation.4 | loop fusion | flops 786432 | bytes 2621444 | tf_op jit(solution)/shard_map/sub | solution.py:12
  (52 shorter events, 1.2 us)
Async XLA Ops:
  0.6 29.1 %copy-start = (f32[512,64]{0,1:T(8,128)S(1)}, f32[512,64]{0,1:T(8,128)}, u32[]{:S(2)}) copy-start(f32[512,64]{0,1:T(8,128)} %param.26) | copy-start | bytes 393220
  0.7 1.8 %copy-start.1 = (f32[2,512,128]{2,1,0:T(8,128)S(1)}, f32[2,512,128]{2,1,0:T(8,128)}, u32[]{:S(2)}) copy-start(f32[2,512,128]{2,1,0:T(8,128)} %param.15) | copy-start | bytes 1572868
  3.8 9.9 %collective-permute-start = (f32[68096]{0:T(1024)S(1)}, f32[68096]{0:T(1024)S(1)}, u32[]{:S(2)}, u32[]{:S(2)}) collective-permute-start(f32[68096]{0:T(1024)S(1)} %dynamic_slice.19), channel_id=1, source_target_pairs={{0,64},{64,0},{128,192},{192,128},{256,320},{320,256},{384,448},{4... | collective-permute-start | bytes 817160 | tf_op jit(solution)/shard_map/ppermute | solution.py:34
  14.0 6.8 %collective-permute-start.1 = (f32[34048]{0:T(1024)S(1)}, f32[34048]{0:T(1024)S(1)}, u32[]{:S(2)}, u32[]{:S(2)}) collective-permute-start(f32[34048]{0:T(1024)S(1)} %dynamic_slice.21), channel_id=1, source_target_pairs={{0,128},{64,192},{128,0},{192,64},{256,384},{320,448},{384,256},{4... | collective-permute-start | bytes 408584 | tf_op jit(solution)/shard_map/ppermute | solution.py:34
  20.7 9.0 %copy-start.5 = (f32[1,125,512]{2,0,1:T(1,128)S(1)}, f32[1,125,512]{2,0,1:T(1,128)}, u32[]{:S(2)}) copy-start(f32[1,125,512]{2,0,1:T(1,128)} %param.23) | copy-start | bytes 768004
  20.9 8.9 %copy-start.3 = (f32[125,512]{1,0:T(8,128)S(1)}, f32[125,512]{1,0:T(8,128)}, u32[]{:S(2)}) copy-start(f32[125,512]{1,0:T(8,128)} %param.24) | copy-start | bytes 768004
  21.0 6.7 %collective-permute-start.2 = (f32[17024]{0:T(1024)S(1)}, f32[17024]{0:T(1024)S(1)}, u32[]{:S(2)}, u32[]{:S(2)}) collective-permute-start(f32[17024]{0:T(1024)S(1)} %dynamic_slice.23), channel_id=1, source_target_pairs={{0,256},{64,320},{128,384},{192,448},{256,0},{320,64},{384,128},{4... | collective-permute-start | bytes 204296 | tf_op jit(solution)/shard_map/ppermute | solution.py:34
  27.8 6.4 %collective-permute-start.3 = (f32[17024]{0:T(1024)S(1)}, f32[17024]{0:T(1024)S(1)}, u32[]{:S(2)}, u32[]{:S(2)}) collective-permute-start(f32[17024]{0:T(1024)S(1)} %dynamic-slice_add_fusion.2), channel_id=1, source_target_pairs={{0,256},{64,320},{128,384},{192,448},{256,0},{320,64},{384,128},{4... | collective-permute-start | bytes 204296 | tf_op jit(solution)/shard_map/ppermute | solution.py:42
  30.1 7.2 %collective-permute-start.6 = (f32[125,64]{0,1:T(8,128)S(1)}, f32[125,64]{0,1:T(8,128)S(1)}, u32[]{:S(2)}, u32[]{:S(2)}) collective-permute-start(f32[125,64]{0,1:T(8,128)S(1)} %fusion.1), channel_id=1, source_target_pairs={{0,64},{64,0},{128,192},{192,128},{256,320},{320,256},{384,448},{4... | collective-permute-start | bytes 96008 | tf_op jit(solution)/shard_map/ppermute | solution.py:23
  34.3 32.0 %collective-permute-start.4 = (f32[34048]{0:T(1024)S(1)}, f32[34048]{0:T(1024)S(1)}, u32[]{:S(2)}, u32[]{:S(2)}) collective-permute-start(f32[34048]{0:T(1024)S(1)} %pad_maximum_fusion.3), channel_id=1, source_target_pairs={{0,128},{64,192},{128,0},{192,64},{256,384},{320,448},{384,256},{4... | collective-permute-start | bytes 408584 | tf_op jit(solution)/shard_map/ppermute | solution.py:42
  37.3 5.1 %collective-permute-start.7 = (f32[125,64]{0,1:T(8,128)S(1)}, f32[125,64]{0,1:T(8,128)S(1)}, u32[]{:S(2)}, u32[]{:S(2)}) collective-permute-start(f32[125,64]{0,1:T(8,128)S(1)} %add.84), channel_id=1, source_target_pairs={{0,128},{64,192},{128,0},{192,64},{256,384},{320,448},{384,256},{4... | collective-permute-start | bytes 96008 | tf_op jit(solution)/shard_map/ppermute | solution.py:23
  42.4 5.5 %collective-permute-start.8 = (f32[125,64]{0,1:T(8,128)S(1)}, f32[125,64]{0,1:T(8,128)S(1)}, u32[]{:S(2)}, u32[]{:S(2)}) collective-permute-start(f32[125,64]{0,1:T(8,128)S(1)} %add.85), channel_id=1, source_target_pairs={{0,256},{64,320},{128,384},{192,448},{256,0},{320,64},{384,128},{4... | collective-permute-start | bytes 96008 | tf_op jit(solution)/shard_map/ppermute | solution.py:23
  47.9 4.6 %collective-permute-start.9 = (f32[125,64]{0,1:T(8,128)S(1)}, f32[125,64]{0,1:T(8,128)S(1)}, u32[]{:S(2)}, u32[]{:S(2)}) collective-permute-start(f32[125,64]{0,1:T(8,128)S(1)} %add.86), channel_id=1, source_target_pairs={{0,1},{1,0},{2,3},{3,2},{4,5},{5,4},{6,7},{7,6},{8,9},{9,8},{10,11... | collective-permute-start | bytes 96008 | tf_op jit(solution)/shard_map/ppermute | solution.py:23
  52.6 6.2 %collective-permute-start.10 = (f32[125,64]{0,1:T(8,128)S(1)}, f32[125,64]{0,1:T(8,128)S(1)}, u32[]{:S(2)}, u32[]{:S(2)}) collective-permute-start(f32[125,64]{0,1:T(8,128)S(1)} %add.87), channel_id=1, source_target_pairs={{0,2},{1,3},{2,0},{3,1},{4,6},{5,7},{6,4},{7,5},{8,10},{9,11},{10,... | collective-permute-start | bytes 96008 | tf_op jit(solution)/shard_map/ppermute | solution.py:23
  58.8 15.5 %collective-permute-start.11 = (f32[125,64]{0,1:T(8,128)S(1)}, f32[125,64]{0,1:T(8,128)S(1)}, u32[]{:S(2)}, u32[]{:S(2)}) collective-permute-start(f32[125,64]{0,1:T(8,128)S(1)} %add.88), channel_id=1, source_target_pairs={{0,4},{1,5},{2,6},{3,7},{4,0},{5,1},{6,2},{7,3},{8,12},{9,13},{10,... | collective-permute-start | bytes 96008 | tf_op jit(solution)/shard_map/ppermute | solution.py:23
  66.3 7.9 %copy-start.6 = (f32[125,512]{1,0:T(8,128)S(1)}, f32[125,512]{1,0:T(8,128)}, u32[]{:S(2)}) copy-start(f32[125,512]{1,0:T(8,128)} %param.25) | copy-start | bytes 768004
  66.4 9.2 %collective-permute-start.5 = (f32[68096]{0:T(1024)S(1)}, f32[68096]{0:T(1024)S(1)}, u32[]{:S(2)}, u32[]{:S(2)}) collective-permute-start(f32[68096]{0:T(1024)S(1)} %pad_maximum_fusion.2), channel_id=1, source_target_pairs={{0,64},{64,0},{128,192},{192,128},{256,320},{320,256},{384,448},{4... | collective-permute-start | bytes 817160 | tf_op jit(solution)/shard_map/ppermute | solution.py:42
  75.7 0.6 copy-start.11
  75.7 3.5 %copy-start.2 = (f32[131072]{0:T(1024)}, f32[131072]{0:T(1024)S(1)}, u32[]{:S(2)}) copy-start(f32[131072]{0:T(1024)S(1)} %fusion) | copy-start | bytes 1572868
  75.8 2.4 %copy-start.4 = (f32[2,512,128]{2,1,0:T(8,128)S(1)}, f32[2,512,128]{2,1,0:T(8,128)}, u32[]{:S(2)}) copy-start(f32[2,512,128]{2,1,0:T(8,128)} %param.16) | copy-start | bytes 1572868
  75.9 0.9 %copy-start.10 = (f32[2,512]{1,0:T(2,128)S(1)}, f32[2,512]{1,0:T(2,128)}, u32[]{:S(2)}) copy-start(f32[2,512]{1,0:T(2,128)} %param.21) | copy-start | bytes 12292
  75.9 0.9 %copy-start.12 = (f32[2,512]{1,0:T(2,128)S(1)}, f32[2,512]{1,0:T(2,128)}, u32[]{:S(2)}) copy-start(f32[2,512]{1,0:T(2,128)} %param.22) | copy-start | bytes 12292
  76.0 1.5 %copy-start.9 = (f32[512,8]{0,1:T(8,128)S(1)}, f32[512,8]{0,1:T(8,128)}, u32[]{:S(2)}) copy-start(f32[512,8]{0,1:T(8,128)} %param.19) | copy-start | bytes 49156
  76.8 1.4 %copy-start.8 = (f32[512,8]{0,1:T(8,128)}, f32[512,8]{0,1:T(8,128)S(1)}, u32[]{:S(2)}) copy-start(f32[512,8]{0,1:T(8,128)S(1)} %copy.36) | copy-start | bytes 49156
  76.8 0.7 copy-start.7

commit v3 on v2

--- a/solution.py
+++ b/solution.py
@@ -4,7 +4,7 @@
 from jax.sharding import PartitionSpec as P
 
 HIGHEST = lax.Precision.HIGHEST
-KV_MODE = "butterfly"
+TENSOR_MODE = "a2a"
 
 
 def nesterov(average, state, anchor, outer_rate):
@@ -48,25 +48,26 @@
           e_local, e_anchor, e_state, basis, rate):
     groups = lax.axis_size("group")
     group_bits = groups.bit_length() - 1
-    tensor_bits = lax.axis_size("tensor").bit_length() - 1
+    tensors = lax.axis_size("tensor")
+    tensor_bits = tensors.bit_length() - 1
     kv_diff = kv_anchor - kv_local[0]
     r_diff = r_anchor - r_local[0]
     g_diff = g_anchor - g_local[0]
     partial = jnp.dot(e_anchor - e_local[0], basis, precision=HIGHEST, preferred_element_type=jnp.float32)
-    steps = [("group", b) for b in range(group_bits)] + [("tensor", b) for b in range(tensor_bits)]
-    factors = all_reduce_doubling(partial, steps)
-    pieces = (kv_diff, r_diff, g_diff)
+    pieces = (kv_diff, r_diff, g_diff, partial)
     flat = jnp.concatenate([p.reshape(-1) for p in pieces])
-    if KV_MODE == "butterfly":
-        bits = list(range(group_bits))
-        total = all_gather_doubling(reduce_scatter_halving(flat, "group", bits), "group", bits[::-1])
-    else:
-        total = lax.psum(flat, "group")
+    bits = list(range(group_bits))
+    total = all_gather_doubling(reduce_scatter_halving(flat, "group", bits), "group", bits[::-1])
     sums, at = [], 0
     for p in pieces:
         sums.append(total[at:at + p.size].reshape(p.shape))
         at += p.size
-    kv_sum, r_sum, g_sum = sums
+    kv_sum, r_sum, g_sum, factors = sums
+    if TENSOR_MODE == "doubling":
+        factors = all_reduce_doubling(factors, [("tensor", b) for b in range(tensor_bits)])
+    else:
+        copies = jnp.broadcast_to(factors[None], (tensors,) + factors.shape)
+        factors = jnp.sum(lax.all_to_all(copies, "tensor", 0, 0, tiled=True), axis=0)
     kv_out = nesterov(kv_sum / groups, kv_state, kv_anchor, rate)
     r_out = nesterov(r_sum / groups, r_state, r_anchor, rate)
     g_out = nesterov(g_sum / groups, g_state, g_anchor, rate)

time: 79.9 us -> 69.7 us (0.87)
  the two profiles are of different devices: /device:TPU:1 before, /device:TPU:48 now
where the time goes in v3:
time: 69.7 us; the launch traced here: 69.2 us
  starting transfers between devices  28.9 us (41%)
  waiting for transfers between devices  28.2 us (40%)
  local copies, waits for them, and re-layouts  4.22 us (6%)
  other arithmetic  3.46 us (5%)
  matrix products  2.78 us (4%)
  between operations  1.59 us (2%)
    ppermute x3, starting transfers between devices, reduce_scatter_halving(): x = keep + lax.ppermute(send, axis, flip(axis, bit))  12.3 us
    ppermute x3, waiting for transfers between devices, all_gather_doubling(): other = lax.ppermute(x, axis, flip(axis, bit))  9.96 us
    ppermute x3, waiting for transfers between devices, reduce_scatter_halving(): x = keep + lax.ppermute(send, axis, flip(axis, bit))  9.31 us
    all_to_all x1, waiting for transfers between devices, local(): lax.all_to_all(copies, 'tensor', 0, 0, tiled=True)  8.92 us
    all_to_all x1, starting transfers between devices, local(): lax.all_to_all(copies, 'tensor', 0, 0, tiled=True)  8.85 us
    ppermute x3, starting transfers between devices, all_gather_doubling(): other = lax.ppermute(x, axis, flip(axis, bit))  7.79 us
    unnamed x32, local copies, waits for them, and re-layouts  2.39 us
    sub x3, other arithmetic, nesterov(): updated = anchor - outer_rate * (average + 0.5 * momentum)  2.29 us
  transfers between devices with their start and end apart: 7, of which 7 were waited for; matrix products, arithmetic and copies ran while one was open for 4% of the time, Pallas kernels for 0%

profile of v3, /device:TPU:48, one launch (start us, length us, event | category | flops | bytes accessed | tf_op | source)
XLA Modules:
  0.0 69.2 jit_solution(15566403699092817503)
XLA Ops:
  0.7 0.7 %copy-done.13 = f32[1,2,512]{2,1,0:T(2,128)S(1)} copy-done((f32[1,2,512]{2,1,0:T(2,128)S(1)}, f32[1,2,512]{2,1,0:T(2,128)}, u32[]{:S(2)}) %copy-start.13) | copy-done | bytes 4120
  1.4 0.2 copy-done
  1.6 1.4 %fusion.1 = f32[125,64]{1,0:T(8,128)S(1)} fusion(f32[512,64]{0,1:T(8,128)S(1)} %copy-done, f32[125,512]{1,0:T(8,128)} %param.24, f32[1,125,512]{2,0,1:T(1,128)} %param.23), kind=kOutput, calls=%fused_computation.9 | convolution fusion | flops 49216000 | bytes 675072 | tf_op jit(solution)/shard_map/dot_general | solution.py:56
  3.1 0.1 copy.52
  3.3 0.2 reshape.55
  3.4 0.6 copy-done.1
  4.2 0.2 dynamic_slice.19
  4.4 1.9 %collective-permute-start = (f32[72096]{0:T(1024)S(1)}, f32[72096]{0:T(1024)S(1)}, u32[]{:S(2)}, u32[]{:S(2)}) collective-permute-start(f32[72096]{0:T(1024)S(1)} %dynamic_slice.19), channel_id=1, source_target_pairs={{0,64},{64,0},{128,192},{192,128},{256,320},{320,256},{384,448},{4... | collective-permute-start | bytes 865160 | tf_op jit(solution)/shard_map/ppermute | solution.py:34
  6.3 1.5 %collective-permute-done = f32[72096]{0:T(1024)S(1)} collective-permute-done((f32[72096]{0:T(1024)S(1)}, f32[72096]{0:T(1024)S(1)}, u32[]{:S(2)}, u32[]{:S(2)}) %collective-permute-start) | collective-permute-done | bytes 288416 | tf_op jit(solution)/shard_map/ppermute | solution.py:34
  7.8 0.1 dynamic-slice_add_fusion
  8.0 0.1 dynamic_slice.21
  8.1 4.3 %collective-permute-start.1 = (f32[36048]{0:T(1024)S(1)}, f32[36048]{0:T(1024)S(1)}, u32[]{:S(2)}, u32[]{:S(2)}) collective-permute-start(f32[36048]{0:T(1024)S(1)} %dynamic_slice.21), channel_id=1, source_target_pairs={{0,128},{64,192},{128,0},{192,64},{256,384},{320,448},{384,256},{4... | collective-permute-start | bytes 432584 | tf_op jit(solution)/shard_map/ppermute | solution.py:34
  12.4 4.1 %collective-permute-done.1 = f32[36048]{0:T(1024)S(1)} collective-permute-done((f32[36048]{0:T(1024)S(1)}, f32[36048]{0:T(1024)S(1)}, u32[]{:S(2)}, u32[]{:S(2)}) %collective-permute-start.1) | collective-permute-done | bytes 144224 | tf_op jit(solution)/shard_map/ppermute | solution.py:34
  16.7 6.1 %collective-permute-start.2 = (f32[18024]{0:T(1024)S(1)}, f32[18024]{0:T(1024)S(1)}, u32[]{:S(2)}, u32[]{:S(2)}) collective-permute-start(f32[18024]{0:T(1024)S(1)} %dynamic_slice.23), channel_id=1, source_target_pairs={{0,256},{64,320},{128,384},{192,448},{256,0},{320,64},{384,128},{4... | collective-permute-start | bytes 216296 | tf_op jit(solution)/shard_map/ppermute | solution.py:34
  22.8 3.7 %collective-permute-done.2 = f32[18024]{0:T(1024)S(1)} collective-permute-done((f32[18024]{0:T(1024)S(1)}, f32[18024]{0:T(1024)S(1)}, u32[]{:S(2)}, u32[]{:S(2)}) %collective-permute-start.2) | collective-permute-done | bytes 72128 | tf_op jit(solution)/shard_map/ppermute | solution.py:34
  26.6 3.6 %collective-permute-start.3 = (f32[18024]{0:T(1024)S(1)}, f32[18024]{0:T(1024)S(1)}, u32[]{:S(2)}, u32[]{:S(2)}) collective-permute-start(f32[18024]{0:T(1024)S(1)} %dynamic-slice_add_fusion.2), channel_id=1, source_target_pairs={{0,256},{64,320},{128,384},{192,448},{256,0},{320,64},{384,128},{4... | collective-permute-start | bytes 216296 | tf_op jit(solution)/shard_map/ppermute | solution.py:42
  30.2 4.3 %collective-permute-done.3 = f32[18024]{0:T(1024)S(1)} collective-permute-done((f32[18024]{0:T(1024)S(1)}, f32[18024]{0:T(1024)S(1)}, u32[]{:S(2)}, u32[]{:S(2)}) %collective-permute-start.3) | collective-permute-done | bytes 72128 | tf_op jit(solution)/shard_map/ppermute | solution.py:42
  34.6 2.3 %collective-permute-start.4 = (f32[36048]{0:T(1024)S(1)}, f32[36048]{0:T(1024)S(1)}, u32[]{:S(2)}, u32[]{:S(2)}) collective-permute-start(f32[36048]{0:T(1024)S(1)} %pad_maximum_fusion.3), channel_id=1, source_target_pairs={{0,128},{64,192},{128,0},{192,64},{256,384},{320,448},{384,256},{4... | collective-permute-start | bytes 432584 | tf_op jit(solution)/shard_map/ppermute | solution.py:42
  36.9 4.7 %collective-permute-done.4 = f32[36048]{0:T(1024)S(1)} collective-permute-done((f32[36048]{0:T(1024)S(1)}, f32[36048]{0:T(1024)S(1)}, u32[]{:S(2)}, u32[]{:S(2)}) %collective-permute-start.4) | collective-permute-done | bytes 144224 | tf_op jit(solution)/shard_map/ppermute | solution.py:42
  41.9 1.9 %collective-permute-start.5 = (f32[72096]{0:T(1024)S(1)}, f32[72096]{0:T(1024)S(1)}, u32[]{:S(2)}, u32[]{:S(2)}) collective-permute-start(f32[72096]{0:T(1024)S(1)} %pad_maximum_fusion.2), channel_id=1, source_target_pairs={{0,64},{64,0},{128,192},{192,128},{256,320},{320,256},{384,448},{4... | collective-permute-start | bytes 865160 | tf_op jit(solution)/shard_map/ppermute | solution.py:42
  44.5 0.9 %collective-permute-done.5 = f32[72096]{0:T(1024)S(1)} collective-permute-done((f32[72096]{0:T(1024)S(1)}, f32[72096]{0:T(1024)S(1)}, u32[]{:S(2)}, u32[]{:S(2)}) %collective-permute-start.5) | collective-permute-done | bytes 288416 | tf_op jit(solution)/shard_map/ppermute | solution.py:42
  45.3 0.1 broadcast_select_fusion.1
  45.7 0.1 fusion
  46.0 0.7 %broadcast_in_dim.8 = f32[8,125,64]{1,2,0:T(8,128)} broadcast(f32[125,64]{0,1:T(8,128)S(1)} %copy.56), dimensions={1,2} | broadcast | bytes 288000 | tf_op jit(solution)/shard_map/broadcast_in_dim | solution.py:69
  46.7 8.8 %all-to-all-start = ((f32[8,125,64]{1,2,0:T(8,128)}), f32[8,125,64]{1,2,0:T(8,128)S(1)}, u32[]{:S(2)}, u32[]{:S(2)}) async-start(f32[8,125,64]{1,2,0:T(8,128)} %broadcast_in_dim.8), calls=%async_computation | async-start | bytes 524288 | tf_op jit(solution)/shard_map/all_to_all | solution.py:70
  55.6 0.2 div.35
  55.9 0.6 copy-done.10
  56.5 0.6 multiply_subtract_fusion.2
  57.2 0.6 multiply_subtract_fusion.3
  57.8 1.1 %multiply_subtract_fusion = (f32[2,512,128]{2,1,0:T(8,128)}, f32[2,512,128]{2,1,0:T(8,128)}) fusion(f32[2,512,128]{2,1,0:T(8,128)S(1)} %copy-done.1, f32[2,512,128]{2,1,0:T(8,128)S(1)} %bitcast.19, f32[]{:T(128)S(6)} %copy.65, f32[2,512,128]{2,1,0:T(8,128)S(1)} %copy-done.5), kind=kLoop, calls=%fused_computation.4 | loop fusion | flops 786432 | bytes 2621444 | tf_op jit(solution)/shard_map/sub | solution.py:12
  58.9 8.9 %all-to-all-done = f32[8,125,64]{1,2,0:T(8,128)S(1)} async-done(((f32[8,125,64]{1,2,0:T(8,128)}), f32[8,125,64]{1,2,0:T(8,128)S(1)}, u32[]{:S(2)}, u32[]{:S(2)}) %all-to-all-start) | async-done | bytes 256032 | tf_op jit(solution)/shard_map/all_to_all | solution.py:70
  67.8 1.3 %multiply_subtract_fusion.1 = (f32[125,512]{1,0:T(8,128)}, f32[125,512]{1,0:T(8,128)}, f32[125,512]{1,0:T(8,128)}) fusion(f32[125,512]{1,0:T(8,128)S(1)} %copy-done.3, f32[]{:T(128)S(6)} %copy.65, f32[125,512]{1,0:T(8,128)S(1)} %copy-done.6, f32[512,64]{0,1:T(8,128)S(1)} %copy-done, f32[125,64]{0,1:T(8,128)S(1)} %reduce_sum.9), kind=kOutput, calls=%fused_computation.11 | convolution fusion | flops 49544000 | bytes 1443076 | tf_op jit(solution)/shard_map/dot_general | solution.py:75
  (47 shorter events, 1.4 us)
Async XLA Ops:
  0.6 0.9 %copy-start = (f32[512,64]{0,1:T(8,128)S(1)}, f32[512,64]{0,1:T(8,128)}, u32[]{:S(2)}) copy-start(f32[512,64]{0,1:T(8,128)} %param.26) | copy-start | bytes 393220
  0.7 0.7 %copy-start.13 = (f32[1,2,512]{2,1,0:T(2,128)S(1)}, f32[1,2,512]{2,1,0:T(2,128)}, u32[]{:S(2)}) copy-start(f32[1,2,512]{2,1,0:T(2,128)} %param.20) | copy-start | bytes 12292
  0.7 0.7 %copy-start.11 = (f32[2,512]{1,0:T(2,128)S(1)}, f32[2,512]{1,0:T(2,128)}, u32[]{:S(2)}) copy-start(f32[2,512]{1,0:T(2,128)} %param.21) | copy-start | bytes 12292
  1.6 1.5 %copy-start.7 = (f32[512,8]{0,1:T(8,128)S(1)}, f32[512,8]{0,1:T(8,128)}, u32[]{:S(2)}) copy-start(f32[512,8]{0,1:T(8,128)} %param.18) | copy-start | bytes 49156
  1.6 1.5 %copy-start.9 = (f32[1,512,8]{1,2,0:T(8,128)S(1)}, f32[1,512,8]{1,2,0:T(8,128)}, u32[]{:S(2)}) copy-start(f32[1,512,8]{1,2,0:T(8,128)} %param.17) | copy-start | bytes 49156
  1.6 1.8 %copy-start.4 = (f32[1,2,512,128]{3,2,1,0:T(8,128)S(1)}, f32[1,2,512,128]{3,2,1,0:T(8,128)}, u32[]{:S(2)}) copy-start(f32[1,2,512,128]{3,2,1,0:T(8,128)} %param.14) | copy-start | bytes 1572868
  3.0 1.0 %copy-start.1 = (f32[2,512,128]{2,1,0:T(8,128)S(1)}, f32[2,512,128]{2,1,0:T(8,128)}, u32[]{:S(2)}) copy-start(f32[2,512,128]{2,1,0:T(8,128)} %param.15) | copy-start | bytes 1572868
  4.4 3.5 %collective-permute-start = (f32[72096]{0:T(1024)S(1)}, f32[72096]{0:T(1024)S(1)}, u32[]{:S(2)}, u32[]{:S(2)}) collective-permute-start(f32[72096]{0:T(1024)S(1)} %dynamic_slice.19), channel_id=1, source_target_pairs={{0,64},{64,0},{128,192},{192,128},{256,320},{320,256},{384,448},{4... | collective-permute-start | bytes 865160 | tf_op jit(solution)/shard_map/ppermute | solution.py:34
  8.1 8.4 %collective-permute-start.1 = (f32[36048]{0:T(1024)S(1)}, f32[36048]{0:T(1024)S(1)}, u32[]{:S(2)}, u32[]{:S(2)}) collective-permute-start(f32[36048]{0:T(1024)S(1)} %dynamic_slice.21), channel_id=1, source_target_pairs={{0,128},{64,192},{128,0},{192,64},{256,384},{320,448},{384,256},{4... | collective-permute-start | bytes 432584 | tf_op jit(solution)/shard_map/ppermute | solution.py:34
  16.7 9.8 %collective-permute-start.2 = (f32[18024]{0:T(1024)S(1)}, f32[18024]{0:T(1024)S(1)}, u32[]{:S(2)}, u32[]{:S(2)}) collective-permute-start(f32[18024]{0:T(1024)S(1)} %dynamic_slice.23), channel_id=1, source_target_pairs={{0,256},{64,320},{128,384},{192,448},{256,0},{320,64},{384,128},{4... | collective-permute-start | bytes 216296 | tf_op jit(solution)/shard_map/ppermute | solution.py:34
  26.6 7.9 %collective-permute-start.3 = (f32[18024]{0:T(1024)S(1)}, f32[18024]{0:T(1024)S(1)}, u32[]{:S(2)}, u32[]{:S(2)}) collective-permute-start(f32[18024]{0:T(1024)S(1)} %dynamic-slice_add_fusion.2), channel_id=1, source_target_pairs={{0,256},{64,320},{128,384},{192,448},{256,0},{320,64},{384,128},{4... | collective-permute-start | bytes 216296 | tf_op jit(solution)/shard_map/ppermute | solution.py:42
  34.6 7.0 %collective-permute-start.4 = (f32[36048]{0:T(1024)S(1)}, f32[36048]{0:T(1024)S(1)}, u32[]{:S(2)}, u32[]{:S(2)}) collective-permute-start(f32[36048]{0:T(1024)S(1)} %pad_maximum_fusion.3), channel_id=1, source_target_pairs={{0,128},{64,192},{128,0},{192,64},{256,384},{320,448},{384,256},{4... | collective-permute-start | bytes 432584 | tf_op jit(solution)/shard_map/ppermute | solution.py:42
  41.9 3.5 %collective-permute-start.5 = (f32[72096]{0:T(1024)S(1)}, f32[72096]{0:T(1024)S(1)}, u32[]{:S(2)}, u32[]{:S(2)}) collective-permute-start(f32[72096]{0:T(1024)S(1)} %pad_maximum_fusion.2), channel_id=1, source_target_pairs={{0,64},{64,0},{128,192},{192,128},{256,320},{320,256},{384,448},{4... | collective-permute-start | bytes 865160 | tf_op jit(solution)/shard_map/ppermute | solution.py:42
  45.7 11.4 %copy-start.12 = (f32[2,512]{1,0:T(2,128)}, f32[2,512]{1,0:T(2,128)S(1)}, u32[]{:S(2)}) copy-start(f32[2,512]{1,0:T(2,128)S(1)} %div.38) | copy-start | bytes 12292
  45.8 11.9 %copy-start.2 = (f32[131072]{0:T(1024)}, f32[131072]{0:T(1024)S(1)}, u32[]{:S(2)}) copy-start(f32[131072]{0:T(1024)S(1)} %fusion) | copy-start | bytes 1572868
  46.7 11.0 %copy-start.5 = (f32[2,512,128]{2,1,0:T(8,128)S(1)}, f32[2,512,128]{2,1,0:T(8,128)}, u32[]{:S(2)}) copy-start(f32[2,512,128]{2,1,0:T(8,128)} %param.16) | copy-start | bytes 1572868
  46.7 21.1 %all-to-all-start = ((f32[8,125,64]{1,2,0:T(8,128)}), f32[8,125,64]{1,2,0:T(8,128)S(1)}, u32[]{:S(2)}, u32[]{:S(2)}) async-start(f32[8,125,64]{1,2,0:T(8,128)} %broadcast_in_dim.8), calls=%async_computation | async-start | bytes 524288 | tf_op jit(solution)/shard_map/all_to_all | solution.py:70
  55.8 0.7 %copy-start.10 = (f32[512,8]{0,1:T(8,128)S(1)}, f32[512,8]{0,1:T(8,128)}, u32[]{:S(2)}) copy-start(f32[512,8]{0,1:T(8,128)} %param.19) | copy-start | bytes 49156
  56.5 0.6 copy-start.8
  56.5 0.7 %copy-start.14 = (f32[2,512]{1,0:T(2,128)S(1)}, f32[2,512]{1,0:T(2,128)}, u32[]{:S(2)}) copy-start(f32[2,512]{1,0:T(2,128)} %param.22) | copy-start | bytes 12292
  57.8 10.0 %copy-start.6 = (f32[125,512]{1,0:T(8,128)S(1)}, f32[125,512]{1,0:T(8,128)}, u32[]{:S(2)}) copy-start(f32[125,512]{1,0:T(8,128)} %param.25) | copy-start | bytes 768004
  58.9 9.0 %copy-start.3 = (f32[125,512]{1,0:T(8,128)S(1)}, f32[125,512]{1,0:T(8,128)}, u32[]{:S(2)}) copy-start(f32[125,512]{1,0:T(8,128)} %param.24) | copy-start | bytes 768004

commit v4 on v2

--- a/solution.py
+++ b/solution.py
@@ -4,7 +4,6 @@
 from jax.sharding import PartitionSpec as P
 
 HIGHEST = lax.Precision.HIGHEST
-KV_MODE = "butterfly"
 
 
 def nesterov(average, state, anchor, outer_rate):
@@ -53,15 +52,34 @@
     r_diff = r_anchor - r_local[0]
     g_diff = g_anchor - g_local[0]
     partial = jnp.dot(e_anchor - e_local[0], basis, precision=HIGHEST, preferred_element_type=jnp.float32)
-    steps = [("group", b) for b in range(group_bits)] + [("tensor", b) for b in range(tensor_bits)]
-    factors = all_reduce_doubling(partial, steps)
+    tile = 1024
+    f = partial.reshape(-1)
+    f = jnp.pad(f, (0, -f.shape[0] % tile))
+    width = f.shape[0]
     pieces = (kv_diff, r_diff, g_diff)
-    flat = jnp.concatenate([p.reshape(-1) for p in pieces])
-    if KV_MODE == "butterfly":
-        bits = list(range(group_bits))
-        total = all_gather_doubling(reduce_scatter_halving(flat, "group", bits), "group", bits[::-1])
-    else:
-        total = lax.psum(flat, "group")
+    x = jnp.concatenate([p.reshape(-1) for p in pieces])
+    x = jnp.pad(x, (0, -x.shape[0] % (groups * tile)))
+    gidx = lax.axis_index("group")
+    bits = list(range(group_bits))
+    for bit in bits:
+        half = x.shape[0] // 2
+        b = (gidx >> bit) & 1
+        keep = lax.dynamic_slice_in_dim(x, b * half, half)
+        send = lax.dynamic_slice_in_dim(x, (1 - b) * half, half)
+        got = lax.ppermute(jnp.concatenate([f, send]), "group", flip("group", bit))
+        f = f + got[:width]
+        x = keep + got[width:]
+    tensor_steps = list(range(tensor_bits))
+    for bit in bits[::-1]:
+        low = ((gidx >> bit) & 1) == 0
+        other = lax.ppermute(x, "group", flip("group", bit))
+        if tensor_steps:
+            t = tensor_steps.pop(0)
+            f = f + lax.ppermute(f, "tensor", flip("tensor", t))
+        x = jnp.concatenate([jnp.where(low, x, other), jnp.where(low, other, x)])
+    for t in tensor_steps:
+        f = f + lax.ppermute(f, "tensor", flip("tensor", t))
+    total = x
     sums, at = [], 0
     for p in pieces:
         sums.append(total[at:at + p.size].reshape(p.shape))
@@ -70,7 +88,7 @@
     kv_out = nesterov(kv_sum / groups, kv_state, kv_anchor, rate)
     r_out = nesterov(r_sum / groups, r_state, r_anchor, rate)
     g_out = nesterov(g_sum / groups, g_state, g_anchor, rate)
-    factors = factors / groups
+    factors = f[:partial.size].reshape(partial.shape) / groups
     e_avg = jnp.dot(factors, basis.T, precision=HIGHEST, preferred_element_type=jnp.float32)
     e_out = nesterov(e_avg, e_state, e_anchor, rate)
     return (*kv_out, *r_out, *g_out, *e_out)

time: 79.9 us -> 68.6 us (0.86)
  starting transfers between devices: 49.4 us -> 33.4 us
  waiting for transfers between devices: 19.1 us -> 24.3 us
  other arithmetic: 5.51 us -> 2.68 us
  local copies, waits for them, and re-layouts: 1.82 us -> 3.22 us
  matrix products: 1.73 us -> 2.72 us
    ppermute x12 -> x9, starting transfers between devices: 49.4 us -> 33.4 us  [the longest x3 12.6 us: local(): got = lax.ppermute(jnp.concatenate([f, send]), 'group', flip('group', bit))]
    ppermute x12 -> x9, waiting for transfers between devices: 19.1 us -> 24.3 us  [the longest x3 14.3 us: local(): got = lax.ppermute(jnp.concatenate([f, send]), 'group', flip('group', bit))]
    unnamed x28 -> x32, local copies, waits for them, and re-layouts: 1.03 us -> 2.57 us
    sub x1, other arithmetic: 1.13 us -> 0.05 us  [local(): kv_diff = kv_anchor - kv_local[0]]
    dot_general x1, matrix products: 0.39 us -> 1.45 us  [local(): jnp.dot(e_anchor - e_local[0], basis, precision=HIGHEST, preferred_elemen...]
  transfers between devices with their start and end apart: 12 -> 9, of which waited for: 7 -> 6; matrix products, arithmetic and copies ran while one was open for 2% -> 2% of each run, Pallas kernels for 0% -> 0%
where the time goes in v4:
time: 68.6 us; the launch traced here: 68.1 us
  starting transfers between devices  33.4 us (49%)
  waiting for transfers between devices  24.3 us (35%)
  local copies, waits for them, and re-layouts  3.22 us (5%)
  matrix products  2.72 us (4%)
  other arithmetic  2.68 us (4%)
  between operations  1.74 us (3%)
    ppermute x3, waiting for transfers between devices, local(): got = lax.ppermute(jnp.concatenate([f, send]), 'group', flip('group', bit))  14.3 us
    ppermute x3, starting transfers between devices, local(): got = lax.ppermute(jnp.concatenate([f, send]), 'group', flip('group', bit))  12.6 us
    ppermute x3, starting transfers between devices, local(): f = f + lax.ppermute(f, 'tensor', flip('tensor', t))  10.7 us
    ppermute x3, starting transfers between devices, local(): other = lax.ppermute(x, 'group', flip('group', bit))  10.2 us
    ppermute x3, waiting for transfers between devices, local(): f = f + lax.ppermute(f, 'tensor', flip('tensor', t))  5.89 us
    ppermute x3, waiting for transfers between devices, local(): other = lax.ppermute(x, 'group', flip('group', bit))  4.08 us
    unnamed x32, local copies, waits for them, and re-layouts  2.57 us
    sub x3, other arithmetic, nesterov(): updated = anchor - outer_rate * (average + 0.5 * momentum)  2.28 us
  transfers between devices with their start and end apart: 9, of which 6 were waited for; matrix products, arithmetic and copies ran while one was open for 2% of the time, Pallas kernels for 0%

profile of v4, /device:TPU:1, one launch (start us, length us, event | category | flops | bytes accessed | tf_op | source)
XLA Modules:
  0.0 68.1 jit_solution(13301452726800524362)
XLA Ops:
  0.7 0.7 %copy-done.13 = f32[1,2,512]{2,1,0:T(2,128)S(1)} copy-done((f32[1,2,512]{2,1,0:T(2,128)S(1)}, f32[1,2,512]{2,1,0:T(2,128)}, u32[]{:S(2)}) %copy-start.13) | copy-done | bytes 4120
  1.4 0.2 copy-done
  1.6 1.4 %fusion.1 = f32[125,64]{1,0:T(8,128)S(1)} fusion(f32[512,64]{0,1:T(8,128)S(1)} %copy-done, f32[125,512]{1,0:T(8,128)} %param.24, f32[1,125,512]{2,0,1:T(1,128)} %param.23), kind=kOutput, calls=%fused_computation.12 | convolution fusion | flops 49216000 | bytes 675072 | tf_op jit(solution)/shard_map/dot_general | solution.py:54
  3.1 0.1 reshape.75
  3.1 0.1 copy.34
  3.3 0.2 reshape.73
  3.5 0.6 copy-done.1
  4.3 8.7 %collective-permute-start = (f32[77824]{0:T(1024)S(1)}, f32[77824]{0:T(1024)S(1)}, u32[]{:S(2)}, u32[]{:S(2)}) collective-permute-start(f32[77824]{0:T(1024)S(1)} %pad_maximum_fusion.1), channel_id=1, source_target_pairs={{0,64},{64,0},{128,192},{192,128},{256,320},{320,256},{384,448},{4... | collective-permute-start | bytes 933896 | tf_op jit(solution)/shard_map/ppermute | solution.py:69
  13.0 1.2 %collective-permute-done = f32[77824]{0:T(1024)S(1)} collective-permute-done((f32[77824]{0:T(1024)S(1)}, f32[77824]{0:T(1024)S(1)}, u32[]{:S(2)}, u32[]{:S(2)}) %collective-permute-start) | collective-permute-done | bytes 311328 | tf_op jit(solution)/shard_map/ppermute | solution.py:69
  14.3 1.9 %collective-permute-start.1 = (f32[43008]{0:T(1024)S(1)}, f32[43008]{0:T(1024)S(1)}, u32[]{:S(2)}, u32[]{:S(2)}) collective-permute-start(f32[43008]{0:T(1024)S(1)} %pad_maximum_fusion.3), channel_id=1, source_target_pairs={{0,128},{64,192},{128,0},{192,64},{256,384},{320,448},{384,256},{4... | collective-permute-start | bytes 516104 | tf_op jit(solution)/shard_map/ppermute | solution.py:69
  16.3 5.5 %collective-permute-done.1 = f32[43008]{0:T(1024)S(1)} collective-permute-done((f32[43008]{0:T(1024)S(1)}, f32[43008]{0:T(1024)S(1)}, u32[]{:S(2)}, u32[]{:S(2)}) %collective-permute-start.1) | collective-permute-done | bytes 172064 | tf_op jit(solution)/shard_map/ppermute | solution.py:69
  21.9 1.9 %collective-permute-start.2 = (f32[25600]{0:T(1024)S(1)}, f32[25600]{0:T(1024)S(1)}, u32[]{:S(2)}, u32[]{:S(2)}) collective-permute-start(f32[25600]{0:T(1024)S(1)} %pad_maximum_fusion.5), channel_id=1, source_target_pairs={{0,256},{64,320},{128,384},{192,448},{256,0},{320,64},{384,128},{4... | collective-permute-start | bytes 307208 | tf_op jit(solution)/shard_map/ppermute | solution.py:69
  23.8 7.6 %collective-permute-done.2 = f32[25600]{0:T(1024)S(1)} collective-permute-done((f32[25600]{0:T(1024)S(1)}, f32[25600]{0:T(1024)S(1)}, u32[]{:S(2)}, u32[]{:S(2)}) %collective-permute-start.2) | collective-permute-done | bytes 102432 | tf_op jit(solution)/shard_map/ppermute | solution.py:69
  31.4 1.9 %collective-permute-start.3 = (f32[17408]{0:T(1024)S(1)}, f32[17408]{0:T(1024)S(1)}, u32[]{:S(2)}, u32[]{:S(2)}) collective-permute-start(f32[17408]{0:T(1024)S(1)} %slice_add_fusion.2), channel_id=1, source_target_pairs={{0,256},{64,320},{128,384},{192,448},{256,0},{320,64},{384,128},{4... | collective-permute-start | bytes 208904 | tf_op jit(solution)/shard_map/ppermute | solution.py:75
  33.4 4.1 %collective-permute-done.3 = f32[17408]{0:T(1024)S(1)} collective-permute-done((f32[17408]{0:T(1024)S(1)}, f32[17408]{0:T(1024)S(1)}, u32[]{:S(2)}, u32[]{:S(2)}) %collective-permute-start.3) | collective-permute-done | bytes 69664 | tf_op jit(solution)/shard_map/ppermute | solution.py:75
  37.5 1.9 %collective-permute-start.4 = (f32[34816]{0:T(1024)S(1)}, f32[34816]{0:T(1024)S(1)}, u32[]{:S(2)}, u32[]{:S(2)}) collective-permute-start(f32[34816]{0:T(1024)S(1)} %pad_maximum_fusion.4), channel_id=1, source_target_pairs={{0,128},{64,192},{128,0},{192,64},{256,384},{320,448},{384,256},{4... | collective-permute-start | bytes 417800 | tf_op jit(solution)/shard_map/ppermute | solution.py:75
  39.4 1.9 %collective-permute-start.6 = (f32[8192]{0:T(1024)S(1)}, f32[8192]{0:T(1024)S(1)}, u32[]{:S(2)}, u32[]{:S(2)}) collective-permute-start(f32[8192]{0:T(1024)S(1)} %slice_add_fusion.4), channel_id=1, source_target_pairs={{0,1},{1,0},{2,3},{3,2},{4,5},{5,4},{6,7},{7,6},{8,9},{9,8},{10,11... | collective-permute-start | bytes 98312 | tf_op jit(solution)/shard_map/ppermute | solution.py:78
  41.3 3.0 %collective-permute-done.6 = f32[8192]{0:T(1024)S(1)} collective-permute-done((f32[8192]{0:T(1024)S(1)}, f32[8192]{0:T(1024)S(1)}, u32[]{:S(2)}, u32[]{:S(2)}) %collective-permute-start.6) | collective-permute-done | bytes 32800 | tf_op jit(solution)/shard_map/ppermute | solution.py:78
  44.4 2.6 %collective-permute-start.7 = (f32[8192]{0:T(1024)S(1)}, f32[8192]{0:T(1024)S(1)}, u32[]{:S(2)}, u32[]{:S(2)}) collective-permute-start(f32[8192]{0:T(1024)S(1)} %add.91), channel_id=1, source_target_pairs={{0,2},{1,3},{2,0},{3,1},{4,6},{5,7},{6,4},{7,5},{8,10},{9,11},{10,... | collective-permute-start | bytes 98312 | tf_op jit(solution)/shard_map/ppermute | solution.py:78
  47.7 2.9 %collective-permute-done.7 = f32[8192]{0:T(1024)S(1)} collective-permute-done((f32[8192]{0:T(1024)S(1)}, f32[8192]{0:T(1024)S(1)}, u32[]{:S(2)}, u32[]{:S(2)}) %collective-permute-start.7) | collective-permute-done | bytes 32800 | tf_op jit(solution)/shard_map/ppermute | solution.py:78
  50.5 6.1 %collective-permute-start.8 = (f32[8192]{0:T(1024)S(1)}, f32[8192]{0:T(1024)S(1)}, u32[]{:S(2)}, u32[]{:S(2)}) collective-permute-start(f32[8192]{0:T(1024)S(1)} %add.92), channel_id=1, source_target_pairs={{0,4},{1,5},{2,6},{3,7},{4,0},{5,1},{6,2},{7,3},{8,12},{9,13},{10,... | collective-permute-start | bytes 98312 | tf_op jit(solution)/shard_map/ppermute | solution.py:78
  56.8 6.3 %collective-permute-start.5 = (f32[69632]{0:T(1024)S(1)}, f32[69632]{0:T(1024)S(1)}, u32[]{:S(2)}, u32[]{:S(2)}) collective-permute-start(f32[69632]{0:T(1024)S(1)} %pad_maximum_fusion.2), channel_id=1, source_target_pairs={{0,64},{64,0},{128,192},{192,128},{256,320},{320,256},{384,448},{4... | collective-permute-start | bytes 835592 | tf_op jit(solution)/shard_map/ppermute | solution.py:75
  63.1 0.1 div.43
  63.2 1.3 %multiply_subtract_fusion.1 = (f32[125,512]{1,0:T(8,128)}, f32[125,512]{1,0:T(8,128)}, f32[125,512]{1,0:T(8,128)}) fusion(f32[125,512]{1,0:T(8,128)S(1)} %copy-done.3, f32[]{:T(128)S(6)} %copy.46, f32[125,512]{1,0:T(8,128)S(1)} %copy-done.6, f32[125,64]{1,0:T(8,128)S(1)} %div.43, f32[512,64]{0,1:T(8,128)S(1)} %copy-done), kind=kOutput, calls=%fused_computation.14 | convolution fusion | flops 49536000 | bytes 1443076 | tf_op jit(solution)/shard_map/dot_general | solution.py:92
  64.6 0.2 div.37
  64.8 0.1 copy.38
  64.9 0.2 copy-done.12
  65.2 0.5 copy-done.14
  65.7 0.6 multiply_subtract_fusion.3
  66.3 0.1 copy-done.10
  66.4 0.6 multiply_subtract_fusion.2
  67.0 1.1 %multiply_subtract_fusion = (f32[2,512,128]{2,1,0:T(8,128)}, f32[2,512,128]{2,1,0:T(8,128)}) fusion(f32[2,512,128]{2,1,0:T(8,128)S(1)} %copy-done.1, f32[2,512,128]{2,1,0:T(8,128)S(1)} %bitcast.20, f32[]{:T(128)S(6)} %copy.46, f32[2,512,128]{2,1,0:T(8,128)S(1)} %copy-done.5), kind=kLoop, calls=%fused_computation.6 | loop fusion | flops 786432 | bytes 2621444 | tf_op jit(solution)/shard_map/sub | solution.py:11
  (57 shorter events, 0.6 us)
Async XLA Ops:
  0.6 0.9 %copy-start = (f32[512,64]{0,1:T(8,128)S(1)}, f32[512,64]{0,1:T(8,128)}, u32[]{:S(2)}) copy-start(f32[512,64]{0,1:T(8,128)} %param.26) | copy-start | bytes 393220
  0.7 0.7 %copy-start.13 = (f32[1,2,512]{2,1,0:T(2,128)S(1)}, f32[1,2,512]{2,1,0:T(2,128)}, u32[]{:S(2)}) copy-start(f32[1,2,512]{2,1,0:T(2,128)} %param.20) | copy-start | bytes 12292
  0.7 0.7 %copy-start.11 = (f32[2,512]{1,0:T(2,128)S(1)}, f32[2,512]{1,0:T(2,128)}, u32[]{:S(2)}) copy-start(f32[2,512]{1,0:T(2,128)} %param.21) | copy-start | bytes 12292
  1.6 1.5 %copy-start.7 = (f32[512,8]{0,1:T(8,128)S(1)}, f32[512,8]{0,1:T(8,128)}, u32[]{:S(2)}) copy-start(f32[512,8]{0,1:T(8,128)} %param.18) | copy-start | bytes 49156
  1.6 1.5 %copy-start.9 = (f32[1,512,8]{1,2,0:T(8,128)S(1)}, f32[1,512,8]{1,2,0:T(8,128)}, u32[]{:S(2)}) copy-start(f32[1,512,8]{1,2,0:T(8,128)} %param.17) | copy-start | bytes 49156
  1.6 1.9 %copy-start.4 = (f32[1,2,512,128]{3,2,1,0:T(8,128)S(1)}, f32[1,2,512,128]{3,2,1,0:T(8,128)}, u32[]{:S(2)}) copy-start(f32[1,2,512,128]{3,2,1,0:T(8,128)} %param.14) | copy-start | bytes 1572868
  3.0 1.0 %copy-start.1 = (f32[2,512,128]{2,1,0:T(8,128)S(1)}, f32[2,512,128]{2,1,0:T(8,128)}, u32[]{:S(2)}) copy-start(f32[2,512,128]{2,1,0:T(8,128)} %param.15) | copy-start | bytes 1572868
  4.3 10.0 %collective-permute-start = (f32[77824]{0:T(1024)S(1)}, f32[77824]{0:T(1024)S(1)}, u32[]{:S(2)}, u32[]{:S(2)}) collective-permute-start(f32[77824]{0:T(1024)S(1)} %pad_maximum_fusion.1), channel_id=1, source_target_pairs={{0,64},{64,0},{128,192},{192,128},{256,320},{320,256},{384,448},{4... | collective-permute-start | bytes 933896 | tf_op jit(solution)/shard_map/ppermute | solution.py:69
  14.3 7.5 %collective-permute-start.1 = (f32[43008]{0:T(1024)S(1)}, f32[43008]{0:T(1024)S(1)}, u32[]{:S(2)}, u32[]{:S(2)}) collective-permute-start(f32[43008]{0:T(1024)S(1)} %pad_maximum_fusion.3), channel_id=1, source_target_pairs={{0,128},{64,192},{128,0},{192,64},{256,384},{320,448},{384,256},{4... | collective-permute-start | bytes 516104 | tf_op jit(solution)/shard_map/ppermute | solution.py:69
  21.9 9.6 %collective-permute-start.2 = (f32[25600]{0:T(1024)S(1)}, f32[25600]{0:T(1024)S(1)}, u32[]{:S(2)}, u32[]{:S(2)}) collective-permute-start(f32[25600]{0:T(1024)S(1)} %pad_maximum_fusion.5), channel_id=1, source_target_pairs={{0,256},{64,320},{128,384},{192,448},{256,0},{320,64},{384,128},{4... | collective-permute-start | bytes 307208 | tf_op jit(solution)/shard_map/ppermute | solution.py:69
  31.4 6.0 %collective-permute-start.3 = (f32[17408]{0:T(1024)S(1)}, f32[17408]{0:T(1024)S(1)}, u32[]{:S(2)}, u32[]{:S(2)}) collective-permute-start(f32[17408]{0:T(1024)S(1)} %slice_add_fusion.2), channel_id=1, source_target_pairs={{0,256},{64,320},{128,384},{192,448},{256,0},{320,64},{384,128},{4... | collective-permute-start | bytes 208904 | tf_op jit(solution)/shard_map/ppermute | solution.py:75
  37.5 19.2 %collective-permute-start.4 = (f32[34816]{0:T(1024)S(1)}, f32[34816]{0:T(1024)S(1)}, u32[]{:S(2)}, u32[]{:S(2)}) collective-permute-start(f32[34816]{0:T(1024)S(1)} %pad_maximum_fusion.4), channel_id=1, source_target_pairs={{0,128},{64,192},{128,0},{192,64},{256,384},{320,448},{384,256},{4... | collective-permute-start | bytes 417800 | tf_op jit(solution)/shard_map/ppermute | solution.py:75
  39.4 5.0 %collective-permute-start.6 = (f32[8192]{0:T(1024)S(1)}, f32[8192]{0:T(1024)S(1)}, u32[]{:S(2)}, u32[]{:S(2)}) collective-permute-start(f32[8192]{0:T(1024)S(1)} %slice_add_fusion.4), channel_id=1, source_target_pairs={{0,1},{1,0},{2,3},{3,2},{4,5},{5,4},{6,7},{7,6},{8,9},{9,8},{10,11... | collective-permute-start | bytes 98312 | tf_op jit(solution)/shard_map/ppermute | solution.py:78
  44.4 6.2 %collective-permute-start.7 = (f32[8192]{0:T(1024)S(1)}, f32[8192]{0:T(1024)S(1)}, u32[]{:S(2)}, u32[]{:S(2)}) collective-permute-start(f32[8192]{0:T(1024)S(1)} %add.91), channel_id=1, source_target_pairs={{0,2},{1,3},{2,0},{3,1},{4,6},{5,7},{6,4},{7,5},{8,10},{9,11},{10,... | collective-permute-start | bytes 98312 | tf_op jit(solution)/shard_map/ppermute | solution.py:78
  50.5 12.6 %collective-permute-start.8 = (f32[8192]{0:T(1024)S(1)}, f32[8192]{0:T(1024)S(1)}, u32[]{:S(2)}, u32[]{:S(2)}) collective-permute-start(f32[8192]{0:T(1024)S(1)} %add.92), channel_id=1, source_target_pairs={{0,4},{1,5},{2,6},{3,7},{4,0},{5,1},{6,2},{7,3},{8,12},{9,13},{10,... | collective-permute-start | bytes 98312 | tf_op jit(solution)/shard_map/ppermute | solution.py:78
  56.7 6.5 %copy-start.3 = (f32[125,512]{1,0:T(8,128)S(1)}, f32[125,512]{1,0:T(8,128)}, u32[]{:S(2)}) copy-start(f32[125,512]{1,0:T(8,128)} %param.24) | copy-start | bytes 768004
  56.7 6.5 %copy-start.6 = (f32[125,512]{1,0:T(8,128)S(1)}, f32[125,512]{1,0:T(8,128)}, u32[]{:S(2)}) copy-start(f32[125,512]{1,0:T(8,128)} %param.25) | copy-start | bytes 768004
  56.8 7.7 %collective-permute-start.5 = (f32[69632]{0:T(1024)S(1)}, f32[69632]{0:T(1024)S(1)}, u32[]{:S(2)}, u32[]{:S(2)}) collective-permute-start(f32[69632]{0:T(1024)S(1)} %pad_maximum_fusion.2), channel_id=1, source_target_pairs={{0,64},{64,0},{128,192},{192,128},{256,320},{320,256},{384,448},{4... | collective-permute-start | bytes 835592 | tf_op jit(solution)/shard_map/ppermute | solution.py:75
  64.6 0.6 copy-start.12
  64.6 3.5 %copy-start.2 = (f32[131072]{0:T(1024)}, f32[131072]{0:T(1024)S(1)}, u32[]{:S(2)}) copy-start(f32[131072]{0:T(1024)S(1)} %fusion) | copy-start | bytes 1572868
  64.6 2.4 %copy-start.5 = (f32[2,512,128]{2,1,0:T(8,128)S(1)}, f32[2,512,128]{2,1,0:T(8,128)}, u32[]{:S(2)}) copy-start(f32[2,512,128]{2,1,0:T(8,128)} %param.16) | copy-start | bytes 1572868
  64.8 0.9 %copy-start.14 = (f32[2,512]{1,0:T(2,128)S(1)}, f32[2,512]{1,0:T(2,128)}, u32[]{:S(2)}) copy-start(f32[2,512]{1,0:T(2,128)} %param.22) | copy-start | bytes 12292
  65.7 1.4 %copy-start.8 = (f32[512,8]{0,1:T(8,128)}, f32[512,8]{0,1:T(8,128)S(1)}, u32[]{:S(2)}) copy-start(f32[512,8]{0,1:T(8,128)S(1)} %copy.38) | copy-start | bytes 49156
  65.7 0.7 %copy-start.10 = (f32[512,8]{0,1:T(8,128)S(1)}, f32[512,8]{0,1:T(8,128)}, u32[]{:S(2)}) copy-start(f32[512,8]{0,1:T(8,128)} %param.19) | copy-start | bytes 49156

commit v5 on v4

--- a/solution.py
+++ b/solution.py
@@ -69,7 +69,7 @@
         got = lax.ppermute(jnp.concatenate([f, send]), "group", flip("group", bit))
         f = f + got[:width]
         x = keep + got[width:]
-    tensor_steps = list(range(tensor_bits))
+    tensor_steps = list(range(tensor_bits))[::-1]
     for bit in bits[::-1]:
         low = ((gidx >> bit) & 1) == 0
         other = lax.ppermute(x, "group", flip("group", bit))

time: 68.6 us -> 68.2 us (level)
  waiting for transfers between devices: 24.3 us -> 23.4 us
    ppermute x3, waiting for transfers between devices: 5.89 us -> 5.01 us  [local(): f = f + lax.ppermute(f, 'tensor', flip('tensor', t))]
where the time goes in v5:
time: 68.2 us; the launch traced here: 67.7 us
  starting transfers between devices  33.9 us (50%)
  waiting for transfers between devices  23.4 us (34%)
  local copies, waits for them, and re-layouts  3.22 us (5%)
  matrix products  2.72 us (4%)
  other arithmetic  2.68 us (4%)
  between operations  1.74 us (3%)
    ppermute x3, waiting for transfers between devices, local(): got = lax.ppermute(jnp.concatenate([f, send]), 'group', flip('group', bit))  14.3 us
    ppermute x3, starting transfers between devices, local(): got = lax.ppermute(jnp.concatenate([f, send]), 'group', flip('group', bit))  12.6 us
    ppermute x3, starting transfers between devices, local(): f = f + lax.ppermute(f, 'tensor', flip('tensor', t))  11.3 us
    ppermute x3, starting transfers between devices, local(): other = lax.ppermute(x, 'group', flip('group', bit))  9.98 us
    ppermute x3, waiting for transfers between devices, local(): f = f + lax.ppermute(f, 'tensor', flip('tensor', t))  5.01 us
    ppermute x3, waiting for transfers between devices, local(): other = lax.ppermute(x, 'group', flip('group', bit))  4.08 us
    unnamed x32, local copies, waits for them, and re-layouts  2.57 us
    sub x3, other arithmetic, nesterov(): updated = anchor - outer_rate * (average + 0.5 * momentum)  2.28 us
  transfers between devices with their start and end apart: 9, of which 6 were waited for; matrix products, arithmetic and copies ran while one was open for 2% of the time, Pallas kernels for 0%

profile of v5, /device:TPU:1, one launch (start us, length us, event | category | flops | bytes accessed | tf_op | source)
XLA Modules:
  0.0 67.7 jit_solution(16032989335176665441)
XLA Ops:
  0.7 0.7 %copy-done.13 = f32[1,2,512]{2,1,0:T(2,128)S(1)} copy-done((f32[1,2,512]{2,1,0:T(2,128)S(1)}, f32[1,2,512]{2,1,0:T(2,128)}, u32[]{:S(2)}) %copy-start.13) | copy-done | bytes 4120
  1.4 0.2 copy-done
  1.6 1.4 %fusion.1 = f32[125,64]{1,0:T(8,128)S(1)} fusion(f32[512,64]{0,1:T(8,128)S(1)} %copy-done, f32[125,512]{1,0:T(8,128)} %param.24, f32[1,125,512]{2,0,1:T(1,128)} %param.23), kind=kOutput, calls=%fused_computation.12 | convolution fusion | flops 49216000 | bytes 675072 | tf_op jit(solution)/shard_map/dot_general | solution.py:54
  3.1 0.1 reshape.75
  3.1 0.1 copy.34
  3.3 0.2 reshape.73
  3.5 0.6 copy-done.1
  4.3 8.7 %collective-permute-start = (f32[77824]{0:T(1024)S(1)}, f32[77824]{0:T(1024)S(1)}, u32[]{:S(2)}, u32[]{:S(2)}) collective-permute-start(f32[77824]{0:T(1024)S(1)} %pad_maximum_fusion.1), channel_id=1, source_target_pairs={{0,64},{64,0},{128,192},{192,128},{256,320},{320,256},{384,448},{4... | collective-permute-start | bytes 933896 | tf_op jit(solution)/shard_map/ppermute | solution.py:69
  13.0 1.2 %collective-permute-done = f32[77824]{0:T(1024)S(1)} collective-permute-done((f32[77824]{0:T(1024)S(1)}, f32[77824]{0:T(1024)S(1)}, u32[]{:S(2)}, u32[]{:S(2)}) %collective-permute-start) | collective-permute-done | bytes 311328 | tf_op jit(solution)/shard_map/ppermute | solution.py:69
  14.3 1.9 %collective-permute-start.1 = (f32[43008]{0:T(1024)S(1)}, f32[43008]{0:T(1024)S(1)}, u32[]{:S(2)}, u32[]{:S(2)}) collective-permute-start(f32[43008]{0:T(1024)S(1)} %pad_maximum_fusion.3), channel_id=1, source_target_pairs={{0,128},{64,192},{128,0},{192,64},{256,384},{320,448},{384,256},{4... | collective-permute-start | bytes 516104 | tf_op jit(solution)/shard_map/ppermute | solution.py:69
  16.3 5.5 %collective-permute-done.1 = f32[43008]{0:T(1024)S(1)} collective-permute-done((f32[43008]{0:T(1024)S(1)}, f32[43008]{0:T(1024)S(1)}, u32[]{:S(2)}, u32[]{:S(2)}) %collective-permute-start.1) | collective-permute-done | bytes 172064 | tf_op jit(solution)/shard_map/ppermute | solution.py:69
  21.9 1.9 %collective-permute-start.2 = (f32[25600]{0:T(1024)S(1)}, f32[25600]{0:T(1024)S(1)}, u32[]{:S(2)}, u32[]{:S(2)}) collective-permute-start(f32[25600]{0:T(1024)S(1)} %pad_maximum_fusion.5), channel_id=1, source_target_pairs={{0,256},{64,320},{128,384},{192,448},{256,0},{320,64},{384,128},{4... | collective-permute-start | bytes 307208 | tf_op jit(solution)/shard_map/ppermute | solution.py:69
  23.8 7.6 %collective-permute-done.2 = f32[25600]{0:T(1024)S(1)} collective-permute-done((f32[25600]{0:T(1024)S(1)}, f32[25600]{0:T(1024)S(1)}, u32[]{:S(2)}, u32[]{:S(2)}) %collective-permute-start.2) | collective-permute-done | bytes 102432 | tf_op jit(solution)/shard_map/ppermute | solution.py:69
  31.4 1.9 %collective-permute-start.3 = (f32[17408]{0:T(1024)S(1)}, f32[17408]{0:T(1024)S(1)}, u32[]{:S(2)}, u32[]{:S(2)}) collective-permute-start(f32[17408]{0:T(1024)S(1)} %slice_add_fusion.2), channel_id=1, source_target_pairs={{0,256},{64,320},{128,384},{192,448},{256,0},{320,64},{384,128},{4... | collective-permute-start | bytes 208904 | tf_op jit(solution)/shard_map/ppermute | solution.py:75
  33.4 4.1 %collective-permute-done.3 = f32[17408]{0:T(1024)S(1)} collective-permute-done((f32[17408]{0:T(1024)S(1)}, f32[17408]{0:T(1024)S(1)}, u32[]{:S(2)}, u32[]{:S(2)}) %collective-permute-start.3) | collective-permute-done | bytes 69664 | tf_op jit(solution)/shard_map/ppermute | solution.py:75
  37.5 1.9 %collective-permute-start.4 = (f32[34816]{0:T(1024)S(1)}, f32[34816]{0:T(1024)S(1)}, u32[]{:S(2)}, u32[]{:S(2)}) collective-permute-start(f32[34816]{0:T(1024)S(1)} %pad_maximum_fusion.4), channel_id=1, source_target_pairs={{0,128},{64,192},{128,0},{192,64},{256,384},{320,448},{384,256},{4... | collective-permute-start | bytes 417800 | tf_op jit(solution)/shard_map/ppermute | solution.py:75
  39.4 6.1 %collective-permute-start.6 = (f32[8192]{0:T(1024)S(1)}, f32[8192]{0:T(1024)S(1)}, u32[]{:S(2)}, u32[]{:S(2)}) collective-permute-start(f32[8192]{0:T(1024)S(1)} %slice_add_fusion.4), channel_id=1, source_target_pairs={{0,4},{1,5},{2,6},{3,7},{4,0},{5,1},{6,2},{7,3},{8,12},{9,13},{10,... | collective-permute-start | bytes 98312 | tf_op jit(solution)/shard_map/ppermute | solution.py:78
  45.6 2.8 %collective-permute-done.6 = f32[8192]{0:T(1024)S(1)} collective-permute-done((f32[8192]{0:T(1024)S(1)}, f32[8192]{0:T(1024)S(1)}, u32[]{:S(2)}, u32[]{:S(2)}) %collective-permute-start.6) | collective-permute-done | bytes 32800 | tf_op jit(solution)/shard_map/ppermute | solution.py:78
  48.3 3.3 %collective-permute-start.7 = (f32[8192]{0:T(1024)S(1)}, f32[8192]{0:T(1024)S(1)}, u32[]{:S(2)}, u32[]{:S(2)}) collective-permute-start(f32[8192]{0:T(1024)S(1)} %add.91), channel_id=1, source_target_pairs={{0,2},{1,3},{2,0},{3,1},{4,6},{5,7},{6,4},{7,5},{8,10},{9,11},{10,... | collective-permute-start | bytes 98312 | tf_op jit(solution)/shard_map/ppermute | solution.py:78
  52.3 2.2 %collective-permute-done.7 = f32[8192]{0:T(1024)S(1)} collective-permute-done((f32[8192]{0:T(1024)S(1)}, f32[8192]{0:T(1024)S(1)}, u32[]{:S(2)}, u32[]{:S(2)}) %collective-permute-start.7) | collective-permute-done | bytes 32800 | tf_op jit(solution)/shard_map/ppermute | solution.py:78
  54.5 1.9 %collective-permute-start.8 = (f32[8192]{0:T(1024)S(1)}, f32[8192]{0:T(1024)S(1)}, u32[]{:S(2)}, u32[]{:S(2)}) collective-permute-start(f32[8192]{0:T(1024)S(1)} %add.92), channel_id=1, source_target_pairs={{0,1},{1,0},{2,3},{3,2},{4,5},{5,4},{6,7},{7,6},{8,9},{9,8},{10,11... | collective-permute-start | bytes 98312 | tf_op jit(solution)/shard_map/ppermute | solution.py:78
  56.5 6.1 %collective-permute-start.5 = (f32[69632]{0:T(1024)S(1)}, f32[69632]{0:T(1024)S(1)}, u32[]{:S(2)}, u32[]{:S(2)}) collective-permute-start(f32[69632]{0:T(1024)S(1)} %pad_maximum_fusion.2), channel_id=1, source_target_pairs={{0,64},{64,0},{128,192},{192,128},{256,320},{320,256},{384,448},{4... | collective-permute-start | bytes 835592 | tf_op jit(solution)/shard_map/ppermute | solution.py:75
  62.7 0.1 div.43
  62.8 1.3 %multiply_subtract_fusion.1 = (f32[125,512]{1,0:T(8,128)}, f32[125,512]{1,0:T(8,128)}, f32[125,512]{1,0:T(8,128)}) fusion(f32[125,512]{1,0:T(8,128)S(1)} %copy-done.3, f32[]{:T(128)S(6)} %copy.46, f32[125,512]{1,0:T(8,128)S(1)} %copy-done.6, f32[125,64]{1,0:T(8,128)S(1)} %div.43, f32[512,64]{0,1:T(8,128)S(1)} %copy-done), kind=kOutput, calls=%fused_computation.14 | convolution fusion | flops 49536000 | bytes 1443076 | tf_op jit(solution)/shard_map/dot_general | solution.py:92
  64.2 0.2 div.37
  64.4 0.1 copy.38
  64.5 0.2 copy-done.12
  64.7 0.5 copy-done.14
  65.2 0.6 multiply_subtract_fusion.3
  65.8 0.1 copy-done.10
  66.0 0.6 multiply_subtract_fusion.2
  66.6 1.1 %multiply_subtract_fusion = (f32[2,512,128]{2,1,0:T(8,128)}, f32[2,512,128]{2,1,0:T(8,128)}) fusion(f32[2,512,128]{2,1,0:T(8,128)S(1)} %copy-done.1, f32[2,512,128]{2,1,0:T(8,128)S(1)} %bitcast.20, f32[]{:T(128)S(6)} %copy.46, f32[2,512,128]{2,1,0:T(8,128)S(1)} %copy-done.5), kind=kLoop, calls=%fused_computation.6 | loop fusion | flops 786432 | bytes 2621444 | tf_op jit(solution)/shard_map/sub | solution.py:11
  (57 shorter events, 0.6 us)
Async XLA Ops:
  0.6 0.9 %copy-start = (f32[512,64]{0,1:T(8,128)S(1)}, f32[512,64]{0,1:T(8,128)}, u32[]{:S(2)}) copy-start(f32[512,64]{0,1:T(8,128)} %param.26) | copy-start | bytes 393220
  0.7 0.7 %copy-start.13 = (f32[1,2,512]{2,1,0:T(2,128)S(1)}, f32[1,2,512]{2,1,0:T(2,128)}, u32[]{:S(2)}) copy-start(f32[1,2,512]{2,1,0:T(2,128)} %param.20) | copy-start | bytes 12292
  0.7 0.7 %copy-start.11 = (f32[2,512]{1,0:T(2,128)S(1)}, f32[2,512]{1,0:T(2,128)}, u32[]{:S(2)}) copy-start(f32[2,512]{1,0:T(2,128)} %param.21) | copy-start | bytes 12292
  1.6 1.5 %copy-start.7 = (f32[512,8]{0,1:T(8,128)S(1)}, f32[512,8]{0,1:T(8,128)}, u32[]{:S(2)}) copy-start(f32[512,8]{0,1:T(8,128)} %param.18) | copy-start | bytes 49156
  1.6 1.5 %copy-start.9 = (f32[1,512,8]{1,2,0:T(8,128)S(1)}, f32[1,512,8]{1,2,0:T(8,128)}, u32[]{:S(2)}) copy-start(f32[1,512,8]{1,2,0:T(8,128)} %param.17) | copy-start | bytes 49156
  1.6 1.9 %copy-start.4 = (f32[1,2,512,128]{3,2,1,0:T(8,128)S(1)}, f32[1,2,512,128]{3,2,1,0:T(8,128)}, u32[]{:S(2)}) copy-start(f32[1,2,512,128]{3,2,1,0:T(8,128)} %param.14) | copy-start | bytes 1572868
  3.0 1.0 %copy-start.1 = (f32[2,512,128]{2,1,0:T(8,128)S(1)}, f32[2,512,128]{2,1,0:T(8,128)}, u32[]{:S(2)}) copy-start(f32[2,512,128]{2,1,0:T(8,128)} %param.15) | copy-start | bytes 1572868
  4.3 10.0 %collective-permute-start = (f32[77824]{0:T(1024)S(1)}, f32[77824]{0:T(1024)S(1)}, u32[]{:S(2)}, u32[]{:S(2)}) collective-permute-start(f32[77824]{0:T(1024)S(1)} %pad_maximum_fusion.1), channel_id=1, source_target_pairs={{0,64},{64,0},{128,192},{192,128},{256,320},{320,256},{384,448},{4... | collective-permute-start | bytes 933896 | tf_op jit(solution)/shard_map/ppermute | solution.py:69
  14.3 7.5 %collective-permute-start.1 = (f32[43008]{0:T(1024)S(1)}, f32[43008]{0:T(1024)S(1)}, u32[]{:S(2)}, u32[]{:S(2)}) collective-permute-start(f32[43008]{0:T(1024)S(1)} %pad_maximum_fusion.3), channel_id=1, source_target_pairs={{0,128},{64,192},{128,0},{192,64},{256,384},{320,448},{384,256},{4... | collective-permute-start | bytes 516104 | tf_op jit(solution)/shard_map/ppermute | solution.py:69
  21.9 9.6 %collective-permute-start.2 = (f32[25600]{0:T(1024)S(1)}, f32[25600]{0:T(1024)S(1)}, u32[]{:S(2)}, u32[]{:S(2)}) collective-permute-start(f32[25600]{0:T(1024)S(1)} %pad_maximum_fusion.5), channel_id=1, source_target_pairs={{0,256},{64,320},{128,384},{192,448},{256,0},{320,64},{384,128},{4... | collective-permute-start | bytes 307208 | tf_op jit(solution)/shard_map/ppermute | solution.py:69
  31.4 6.0 %collective-permute-start.3 = (f32[17408]{0:T(1024)S(1)}, f32[17408]{0:T(1024)S(1)}, u32[]{:S(2)}, u32[]{:S(2)}) collective-permute-start(f32[17408]{0:T(1024)S(1)} %slice_add_fusion.2), channel_id=1, source_target_pairs={{0,256},{64,320},{128,384},{192,448},{256,0},{320,64},{384,128},{4... | collective-permute-start | bytes 208904 | tf_op jit(solution)/shard_map/ppermute | solution.py:75
  37.5 18.9 %collective-permute-start.4 = (f32[34816]{0:T(1024)S(1)}, f32[34816]{0:T(1024)S(1)}, u32[]{:S(2)}, u32[]{:S(2)}) collective-permute-start(f32[34816]{0:T(1024)S(1)} %pad_maximum_fusion.4), channel_id=1, source_target_pairs={{0,128},{64,192},{128,0},{192,64},{256,384},{320,448},{384,256},{4... | collective-permute-start | bytes 417800 | tf_op jit(solution)/shard_map/ppermute | solution.py:75
  39.4 8.9 %collective-permute-start.6 = (f32[8192]{0:T(1024)S(1)}, f32[8192]{0:T(1024)S(1)}, u32[]{:S(2)}, u32[]{:S(2)}) collective-permute-start(f32[8192]{0:T(1024)S(1)} %slice_add_fusion.4), channel_id=1, source_target_pairs={{0,4},{1,5},{2,6},{3,7},{4,0},{5,1},{6,2},{7,3},{8,12},{9,13},{10,... | collective-permute-start | bytes 98312 | tf_op jit(solution)/shard_map/ppermute | solution.py:78
  48.3 6.2 %collective-permute-start.7 = (f32[8192]{0:T(1024)S(1)}, f32[8192]{0:T(1024)S(1)}, u32[]{:S(2)}, u32[]{:S(2)}) collective-permute-start(f32[8192]{0:T(1024)S(1)} %add.91), channel_id=1, source_target_pairs={{0,2},{1,3},{2,0},{3,1},{4,6},{5,7},{6,4},{7,5},{8,10},{9,11},{10,... | collective-permute-start | bytes 98312 | tf_op jit(solution)/shard_map/ppermute | solution.py:78
  54.5 8.2 %collective-permute-start.8 = (f32[8192]{0:T(1024)S(1)}, f32[8192]{0:T(1024)S(1)}, u32[]{:S(2)}, u32[]{:S(2)}) collective-permute-start(f32[8192]{0:T(1024)S(1)} %add.92), channel_id=1, source_target_pairs={{0,1},{1,0},{2,3},{3,2},{4,5},{5,4},{6,7},{7,6},{8,9},{9,8},{10,11... | collective-permute-start | bytes 98312 | tf_op jit(solution)/shard_map/ppermute | solution.py:78
  56.5 6.3 %copy-start.3 = (f32[125,512]{1,0:T(8,128)S(1)}, f32[125,512]{1,0:T(8,128)}, u32[]{:S(2)}) copy-start(f32[125,512]{1,0:T(8,128)} %param.24) | copy-start | bytes 768004
  56.5 6.3 %copy-start.6 = (f32[125,512]{1,0:T(8,128)S(1)}, f32[125,512]{1,0:T(8,128)}, u32[]{:S(2)}) copy-start(f32[125,512]{1,0:T(8,128)} %param.25) | copy-start | bytes 768004
  56.5 7.5 %collective-permute-start.5 = (f32[69632]{0:T(1024)S(1)}, f32[69632]{0:T(1024)S(1)}, u32[]{:S(2)}, u32[]{:S(2)}) collective-permute-start(f32[69632]{0:T(1024)S(1)} %pad_maximum_fusion.2), channel_id=1, source_target_pairs={{0,64},{64,0},{128,192},{192,128},{256,320},{320,256},{384,448},{4... | collective-permute-start | bytes 835592 | tf_op jit(solution)/shard_map/ppermute | solution.py:75
  64.1 0.6 copy-start.12
  64.2 3.5 %copy-start.2 = (f32[131072]{0:T(1024)}, f32[131072]{0:T(1024)S(1)}, u32[]{:S(2)}) copy-start(f32[131072]{0:T(1024)S(1)} %fusion) | copy-start | bytes 1572868
  64.2 2.4 %copy-start.5 = (f32[2,512,128]{2,1,0:T(8,128)S(1)}, f32[2,512,128]{2,1,0:T(8,128)}, u32[]{:S(2)}) copy-start(f32[2,512,128]{2,1,0:T(8,128)} %param.16) | copy-start | bytes 1572868
  64.4 0.9 %copy-start.14 = (f32[2,512]{1,0:T(2,128)S(1)}, f32[2,512]{1,0:T(2,128)}, u32[]{:S(2)}) copy-start(f32[2,512]{1,0:T(2,128)} %param.22) | copy-start | bytes 12292
  65.2 1.4 %copy-start.8 = (f32[512,8]{0,1:T(8,128)}, f32[512,8]{0,1:T(8,128)S(1)}, u32[]{:S(2)}) copy-start(f32[512,8]{0,1:T(8,128)S(1)} %copy.38) | copy-start | bytes 49156
  65.2 0.7 %copy-start.10 = (f32[512,8]{0,1:T(8,128)S(1)}, f32[512,8]{0,1:T(8,128)}, u32[]{:S(2)}) copy-start(f32[512,8]{0,1:T(8,128)} %param.19) | copy-start | bytes 49156
